TPU v7x, 128 devices: a whole 4x4x4 slice. The times are simulated.
128 devices in a mesh: row: 4 (over z), col: 32 (over y, x, core).
Axes of the slice: x: 4, y: 4, z: 4, core: 2. Of those that a mesh axis runs over, the one named last changes fastest.
Arguments:
- pooled: bfloat16 [49152, 1024], P(('row', 'col')), may hold values from -6 to 6
- enc_weight: bfloat16 [1024, 1024], replicated, may hold values from -0.1875 to 0.1875
- norm_gain: float32 [1024], replicated, may hold values from 0.1 to 1.9
- shortlist: int32 [49152, 16], P(('row', 'col')), may hold values from 0 to 1535, all different within a row; in each aligned block of 384 rows (0 to 383, 384 to 767, ...) at most 6 rows name the same one
- positives: int32 [49152, 8], P(('row', 'col')), may hold values from 0 to 4095
- label_weight: bfloat16 [256, 1536, 1024], P(None, ('row', 'col')), may hold values from -0.1875 to 0.1875
Outputs:
- query_grad: float32 [49152, 1024], P(('row', 'col'))
- weight_grad: float32 [256, 1536, 1024], P(None, ('row', 'col'))
Inputs may be any that keep to these rules, and one draw needn't show every extreme that they name: `shortlist`: the 16 clusters of a query differ. Among the 384 queries of one device (aligned blocks of rows) no cluster is named more than 6 times, a bound that some block reaches. Every cluster is named by some query. Cluster c is held by the device of index c // 12 along row+col.
All inputs are finite; a program needn't handle non-finite values.
Results may differ from a plain program's by a relative error of at most 0.0038.
Values may be sent and summed in bfloat16 or wider, within the bound.
No kernel may reach another device: no remote copies, remote signals or barrier semaphores. Data moves between devices by JAX's collectives and lax.ppermute only.
A program may use at most 256 MiB of HBM per device.

v0:
```python
import jax
import jax.numpy as jnp
from jax import lax
from jax.sharding import PartitionSpec as P

CAP = 6


def encode(pooled, enc_weight, norm_gain):
    projected = jnp.dot(pooled, enc_weight, preferred_element_type=jnp.float32)
    average = jnp.mean(projected, axis=-1, keepdims=True)
    centred = projected - average
    spread = jnp.mean(centred * centred, axis=-1, keepdims=True)
    return (centred * lax.rsqrt(spread + 1e-05) * norm_gain).astype(jnp.bfloat16)


def slot_ranks(cluster_ids):
    position = jnp.arange(cluster_ids.shape[0], dtype=jnp.int32)
    same = cluster_ids[:, None] == cluster_ids[None, :]
    earlier = position[:, None] > position[None, :]
    return jnp.sum((same & earlier).astype(jnp.int32), axis=1)


def on_device(pooled, enc_weight, norm_gain, shortlist, positives, label_weight):
    queries = encode(pooled, enc_weight, norm_gain)
    row_count = lax.axis_size("row")
    col_count = lax.axis_size("col")
    devices = row_count * col_count
    width = queries.shape[1]
    query_count = queries.shape[0]
    block_labels = label_weight.shape[0]
    local_clusters = label_weight.shape[1]
    shortlist_size = shortlist.shape[1]
    positive_count = positives.shape[1]
    slot_total = devices * local_clusters * CAP
    cluster_ids = shortlist.reshape(-1)
    slot_index = cluster_ids * CAP + slot_ranks(cluster_ids)
    query_rows = jnp.repeat(queries, shortlist_size, axis=0)
    outgoing = jnp.zeros((slot_total, width), jnp.bfloat16).at[slot_index].set(query_rows)
    outgoing = outgoing.reshape(devices, local_clusters, CAP, width)
    offsets = (
        positives[:, None, :]
        - (jnp.arange(shortlist_size, dtype=jnp.int32) * block_labels)[None, :, None]
    )
    inside = (offsets >= 0) & (offsets < block_labels)
    local_positive = jnp.where(inside, offsets, -1).reshape(-1, positive_count)
    outgoing_pos = (
        jnp.full((slot_total, positive_count), -1, jnp.int32).at[slot_index].set(local_positive)
    )
    outgoing_pos = outgoing_pos.reshape(devices, local_clusters, CAP, positive_count)
    incoming, incoming_pos = (
        lax.all_to_all(outgoing, ("row", "col"), split_axis=0, concat_axis=0, tiled=True),
        lax.all_to_all(outgoing_pos, ("row", "col"), split_axis=0, concat_axis=0, tiled=True),
    )
    scores = jnp.einsum(
        "scxd,jcd->scxj", incoming, label_weight, preferred_element_type=jnp.float32
    )
    labels = jnp.arange(block_labels, dtype=jnp.int32)
    target = jnp.zeros(scores.shape, jnp.bool_)
    for column in range(positive_count):
        target = target | (incoming_pos[..., column : column + 1] == labels)
    signal = (jax.nn.sigmoid(scores) - target.astype(jnp.float32)).astype(jnp.bfloat16)
    weight_grad = jnp.einsum("scxj,scxd->jcd", signal, incoming, preferred_element_type=jnp.float32)
    row_grads = jnp.einsum(
        "scxj,jcd->scxd", signal, label_weight, preferred_element_type=jnp.float32
    ).astype(jnp.bfloat16)
    returned = lax.all_to_all(row_grads, ("row", "col"), split_axis=0, concat_axis=0, tiled=True)
    returned = returned.reshape(slot_total, width)
    picked = returned[slot_index].astype(jnp.float32).reshape(query_count, shortlist_size, width)
    return (jnp.sum(picked, axis=1), weight_grad)


def solution(mesh):
    in_specs = (
        P(("row", "col"), None),
        P(),
        P(),
        P(("row", "col"), None),
        P(("row", "col"), None),
        P(None, ("row", "col"), None),
    )
    out_specs = (P(("row", "col"), None), P(None, ("row", "col"), None))
    return jax.shard_map(
        on_device, mesh=mesh, in_specs=in_specs, out_specs=out_specs, check_vma=False
    )
```

profile of v0, /device:TPU:10, one launch (start us, length us, event | category | flops | bytes accessed | tf_op | source)
XLA Modules:
  0.0 1130.3 jit_solution(11338480145541913613)
XLA Ops:
  0.6 0.0 copy-start
  0.7 0.9 broadcast_multiply_fusion
  1.5 0.9 copy.76
  2.4 0.1 copy.75
  2.5 0.1 mul.44
  2.7 0.1 sub.36
  2.8 0.1 eq.135
  2.9 42.8 %convert_reduce_fusion = s32[6144]{0:T(1024)S(1)} fusion(s32[6144]{0:T(1024)S(1)} %eq.135), kind=kLoop, calls=%fused_computation.3 | loop fusion | flops 188737536 | bytes 49152 | tf_op jit(solution)/shard_map/reduce_sum | solution.py:21
  45.8 2.2 sub.33
  47.9 2.5 sub.34
  50.4 2.2 copy.78
  52.6 18.3 %scatter_custom_fusion.1 = s32[9216,8]{1,0:T(8,128)} fusion(s32[6144]{0:T(1024)S(1)} %bitcast.49, s32[6144,8]{1,0:T(8,128)} %copy.78, s32[]{:T(128)} %constant.6.clone.1), kind=kCustom, calls=%fused_computation.31 | custom fusion | bytes 295424 | tf_op jit(solution)/shard_map/scatter | solution.py:48
  70.9 6.5 reshape.103
  77.4 0.0 copy-start.3
  77.4 0.0 copy-start.2
  77.4 7.7 copy.80
  85.1 4.2 reshape.108
  89.4 10.8 all-to-all-start.1
  100.2 0.0 copy-done
  100.2 0.0 copy-done.3
  100.2 1.1 fusion.19
  101.3 0.3 multiply_reduce_fusion
  101.6 0.0 copy-done.2
  101.6 0.3 multiply_convert_fusion
  101.9 5.5 broadcast_in_dim.10
  107.4 39.2 %scatter_custom_fusion = bf16[9216,1024]{1,0:T(8,128)(2,1)} fusion(s32[6144]{0:T(1024)S(1)} %bitcast.50, bf16[6144,1024]{1,0:T(8,128)(2,1)} %bitcast.46, bf16[]{:T(256)} %constant.11.clone.1), kind=kCustom, calls=%fused_computation.18 | custom fusion | bytes 18874880 | tf_op jit(solution)/shard_map/scatter | solution.py:39
  146.6 30.0 %reshape.73 = bf16[128,12,6,1024]{3,2,1,0:T(8,128)(2,1)} reshape(bf16[9216,1024]{1,0:T(8,128)(2,1)} %scatter_custom_fusion) | data formatting | bytes 37748736 | tf_op jit(solution)/shard_map/reshape | solution.py:40
  176.7 0.0 all-to-all-done.1
  176.7 10.5 all-to-all-start
  187.2 0.5 broadcast.86
  187.7 1.4 reduce
  189.1 3.5 reshape.109
  192.6 12.9 %fusion.18 = (s32[128,12,6,1]{1,3,2,0:T(1,128)S(1)}, s32[128,12,6,1]{1,3,2,0:T(1,128)S(1)}, s32[128,12,6,1]{1,3,2,0:T(1,128)S(1)}, s32[128,12,6,1]{1,3,2,0:T(1,1...) fusion(s32[128,12,6,8]{1,3,2,0:T(8,128)} %bitcast.47), kind=kLoop, calls=%fused_computation.42 | loop fusion | bytes 589824 | tf_op jit(solution)/shard_map/slice | solution.py:61
  205.5 0.2 copy.96
  205.7 0.2 copy.102
  205.9 0.2 copy.101
  206.1 0.2 copy.100
  206.4 0.2 copy.99
  206.6 0.2 copy.98
  206.8 0.2 copy.97
  207.0 0.2 copy.103
  207.2 359.3 %all-to-all-done = bf16[128,12,6,1024]{3,2,1,0:T(8,128)(2,1)} async-done(((bf16[128,12,6,1024]{3,2,1,0:T(8,128)(2,1)}), bf16[128,12,6,1024]{3,2,1,0:T(8,128)(2,1)}, u32[]{:S(2)}, u32[]{:S(2)}) %all-to-all-start) | async-done | bytes 18874400 | tf_op jit(solution)/shard_map/all_to_all | solution.py:52
  566.5 29.9 %copy.90 = bf16[128,12,6,1024]{0,3,2,1:T(8,128)(2,1)} copy(bf16[128,12,6,1024]{3,2,1,0:T(8,128)(2,1)} %all-to-all-done) | data formatting | bytes 37748736 | tf_op jit(solution)/shard_map/all_to_all | solution.py:52
  596.4 19.5 %fusion.1 = bf16[128,12,6,256]{3,0,2,1:T(8,128)(2,1)} fusion(s32[128,12,6]{0,2,1:T(8,128)S(1)} %bitcast.59, s32[128,12,6]{0,2,1:T(8,128)S(1)} %bitcast.53, s32[128,12,6]{0,2,1:T(8,128)S(1)} %bitcast.54, s32[128,12,6]{0,2,1:T(8,128)S(1)} %bitcast.55, s32[128,12,6]{0,2,1:T(8,128)S(1)} %bitcast.56, s32[128,12,6]{0,2,1:T(8,128)S(1)} %bitcast.57, ...), kind=kOutput, calls=%fused_computation.9 | convolution fusion | flops 4881383424 | bytes 30179328 | tf_op jit(solution)/shard_map/scxd,jcd->scxj/dot_general | solution.py:55
  615.9 12.4 %convert_bitcast_fusion = bf16[128,12,6,1024]{3,0,2,1:T(8,128)(2,1)} fusion(bf16[128,12,6,256]{3,0,2,1:T(8,128)(2,1)} %fusion.1, bf16[256,12,1024]{2,0,1:T(8,128)(2,1)} %param.11), kind=kOutput, calls=%fused_computation.7 | convolution fusion | flops 4841275392 | bytes 29884416 | tf_op jit(solution)/shard_map/scxj,jcd->scxd/dot_general | solution.py:64
  628.3 20.4 %copy.89 = bf16[128,12,6,1024]{3,2,1,0:T(8,128)(2,1)} copy(bf16[128,12,6,1024]{3,0,2,1:T(8,128)(2,1)} %convert_bitcast_fusion) | data formatting | bytes 37748736 | tf_op jit(solution)/shard_map/convert_element_type | solution.py:66
  648.7 22.3 %all-to-all-start.2 = ((bf16[128,12,6,1024]{3,2,1,0:T(8,128)(2,1)}), bf16[128,12,6,1024]{3,2,1,0:T(8,128)(2,1)}, u32[]{:S(2)}, u32[]{:S(2)}) async-start(bf16[128,12,6,1024]{3,2,1,0:T(8,128)(2,1)} %copy.89), calls=%async_computation.2 | async-start | bytes 50331648 | tf_op jit(solution)/shard_map/all_to_all | solution.py:67
  671.0 13.0 %convolution_bitcast_fusion = f32[256,12,1024]{0,2,1:T(8,128)} fusion(bf16[128,12,6,1024]{0,3,2,1:T(8,128)(2,1)} %copy.90, bf16[128,12,6,256]{3,0,2,1:T(8,128)(2,1)} %fusion.1), kind=kOutput, calls=%fused_computation.30 | convolution fusion | flops 4831838208 | bytes 36175872 | tf_op jit(solution)/shard_map/scxj,scxd->jcd/dot_general | solution.py:63
  684.0 12.6 %copy.91 = f32[256,12,1024]{2,0,1:T(8,128)} copy(f32[256,12,1024]{0,2,1:T(8,128)} %convolution_bitcast_fusion) | data formatting | bytes 25165824
  696.6 353.7 %all-to-all-done.2 = bf16[128,12,6,1024]{3,2,1,0:T(8,128)(2,1)} async-done(((bf16[128,12,6,1024]{3,2,1,0:T(8,128)(2,1)}), bf16[128,12,6,1024]{3,2,1,0:T(8,128)(2,1)}, u32[]{:S(2)}, u32[]{:S(2)}) %all-to-all-start.2) | async-done | bytes 18874400 | tf_op jit(solution)/shard_map/all_to_all | solution.py:67
  1050.4 30.3 %reshape.75 = bf16[9216,1024]{1,0:T(8,128)(2,1)} reshape(bf16[128,12,6,1024]{3,2,1,0:T(8,128)(2,1)} %all-to-all-done.2) | data formatting | bytes 37748736 | tf_op jit(solution)/shard_map/reshape | solution.py:68
  1080.7 0.0 copy-start.1
  1080.7 39.7 %gather_fusion = bf16[6144,1024]{1,0:T(8,128)(2,1)} fusion(bf16[9216,1024]{1,0:T(8,128)(2,1)} %reshape.75, s32[6144]{0:T(1024)S(1)} %broadcast_clamp_fusion), kind=kCustom, calls=%fused_computation | custom fusion | bytes 25190400 | tf_op jit(solution)/shard_map/gather | solution.py:69
  1120.4 9.7 convert_reduce_fusion.1
  1130.1 0.0 copy-done.1
  (7 shorter events, 0.1 us)
Async XLA Ops:
  0.6 99.6 %copy-start = (bf16[1024,1024]{1,0:T(8,128)(2,1)S(1)}, bf16[1024,1024]{1,0:T(8,128)(2,1)}, u32[]{:S(2)}) copy-start(bf16[1024,1024]{1,0:T(8,128)(2,1)} %param.7) | copy-start | bytes 6291460
  77.4 22.8 %copy-start.3 = (bf16[384,1024]{1,0:T(8,128)(2,1)S(1)}, bf16[384,1024]{1,0:T(8,128)(2,1)}, u32[]{:S(2)}) copy-start(bf16[384,1024]{1,0:T(8,128)(2,1)} %param.6) | copy-start | bytes 2359300
  77.4 24.2 %copy-start.2 = (f32[1024]{0:T(1024)S(1)}, f32[1024]{0:T(1024)}, u32[]{:S(2)}) copy-start(f32[1024]{0:T(1024)} %param.8) | copy-start | bytes 12292
  89.4 87.3 %all-to-all-start.1 = ((s32[128,1,576]{2,1,0:T(1,128)}), s32[128,1,576]{2,1,0:T(1,128)S(1)}, u32[]{:S(2)}, u32[]{:S(2)}) async-start(s32[128,1,576]{2,1,0:T(1,128)} %reshape.108), calls=%async_computation.1 | async-start | bytes 655360 | tf_op jit(solution)/shard_map/all_to_all | solution.py:53
  176.7 389.9 %all-to-all-start = ((bf16[128,12,6,1024]{3,2,1,0:T(8,128)(2,1)}), bf16[128,12,6,1024]{3,2,1,0:T(8,128)(2,1)}, u32[]{:S(2)}, u32[]{:S(2)}) async-start(bf16[128,12,6,1024]{3,2,1,0:T(8,128)(2,1)} %reshape.73), calls=%async_computation | async-start | bytes 50331648 | tf_op jit(solution)/shard_map/all_to_all | solution.py:52
  648.7 401.6 %all-to-all-start.2 = ((bf16[128,12,6,1024]{3,2,1,0:T(8,128)(2,1)}), bf16[128,12,6,1024]{3,2,1,0:T(8,128)(2,1)}, u32[]{:S(2)}, u32[]{:S(2)}) async-start(bf16[128,12,6,1024]{3,2,1,0:T(8,128)(2,1)} %copy.89), calls=%async_computation.2 | async-start | bytes 50331648 | tf_op jit(solution)/shard_map/all_to_all | solution.py:67
  1080.7 49.4 %copy-start.1 = (bf16[1024,1024]{1,0:T(8,128)(2,1)S(1)}, bf16[1024,1024]{1,0:T(8,128)(2,1)}, u32[]{:S(2)}) copy-start(bf16[1024,1024]{1,0:T(8,128)(2,1)} %param.7) | copy-start | bytes 6291460
where the time goes:
time: 1150 us; the launch traced here: 1130 us
  waiting for transfers between devices  713 us (62%)
  local copies, waits for them, and re-layouts  271 us (24%)
  other arithmetic  55.5 us (5%)
  matrix products  46 us (4%)
  starting transfers between devices  43.6 us (4%)
    all_to_all x1, waiting for transfers between devices, on_device(): lax.all_to_all(outgoing, ('row', 'col'), split_axis=0, concat_axis=0, til...  359 us
    all_to_all x1, waiting for transfers between devices, on_device(): lax.all_to_all(row_grads, ('row', 'col'), split_axis=0, concat_axis=0, ti...  354 us
    reduce_sum x1, other arithmetic, slot_ranks(): return jnp.sum((same & earlier).astype(jnp.int32), axis=1)  42.8 us
    gather x1, local copies, waits for them, and re-layouts, on_device(): returned[slot_index].astype(jnp.float32)  39.7 us
    scatter x1, local copies, waits for them, and re-layouts, on_device(): jnp.zeros((slot_total, width), jnp.bfloat16).at[slot_index].set(query_rows)  39.2 us
    reshape x1, local copies, waits for them, and re-layouts, on_device(): returned = returned.reshape(slot_total, width)  30.3 us
    reshape x1, local copies, waits for them, and re-layouts, on_device(): outgoing = outgoing.reshape(devices, local_clusters, CAP, width)  30 us
    all_to_all x1, local copies, waits for them, and re-layouts, on_device(): lax.all_to_all(outgoing, ('row', 'col'), split_axis=0, concat_axis=0, til...  29.9 us
  transfers between devices with their start and end apart: 3, of which 2 were waited for; matrix products, arithmetic and copies ran while one was open for 11% of the time, Pallas kernels for 0%

commit v1 on v0

v1 whole, which is shorter than its diff:
```python
import jax
import jax.numpy as jnp
from jax import lax
from jax.sharding import PartitionSpec as P

CAP = 6
AXES = ("row", "col")


def encode(pooled, enc_weight, norm_gain):
    projected = jnp.dot(pooled, enc_weight, preferred_element_type=jnp.float32)
    average = jnp.mean(projected, axis=-1, keepdims=True)
    centred = projected - average
    spread = jnp.mean(centred * centred, axis=-1, keepdims=True)
    return (centred * lax.rsqrt(spread + 1e-05) * norm_gain).astype(jnp.bfloat16)


def on_device(pooled, enc_weight, norm_gain, shortlist, positives, label_weight):
    queries = encode(pooled, enc_weight, norm_gain)
    devices = lax.axis_size("row") * lax.axis_size("col")
    query_count, width = queries.shape
    block_labels, local_clusters, _ = label_weight.shape
    shortlist_size = shortlist.shape[1]
    positive_count = positives.shape[1]
    clusters = devices * local_clusters
    slots = clusters * CAP

    cluster_id = jnp.arange(clusters, dtype=jnp.int32)
    hit = shortlist.T[:, None, :] == cluster_id[None, :, None]
    member = jnp.any(hit, axis=0)
    position = jnp.sum(
        jnp.where(hit, jnp.arange(shortlist_size, dtype=jnp.int32)[:, None, None], 0), axis=0
    )
    earlier = (
        jnp.arange(query_count, dtype=jnp.int32)[:, None]
        < jnp.arange(query_count, dtype=jnp.int32)[None, :]
    ).astype(jnp.bfloat16)
    rank = jnp.dot(member.astype(jnp.bfloat16), earlier, preferred_element_type=jnp.float32)
    slot_of = jnp.arange(CAP, dtype=jnp.float32)
    dispatch = member[:, None, :] & (rank[:, None, :] == slot_of[None, :, None])
    dispatch = dispatch.astype(jnp.bfloat16).reshape(slots, query_count)

    outgoing = jnp.dot(dispatch, queries, preferred_element_type=jnp.float32).astype(jnp.bfloat16)
    split = jnp.concatenate([positives // 256, positives % 256], axis=1).astype(jnp.bfloat16)
    gathered = jnp.dot(dispatch, split, preferred_element_type=jnp.float32)
    raw = (gathered[:, :positive_count] * 256 + gathered[:, positive_count:]).astype(jnp.int32)
    picked = dispatch.reshape(clusters, CAP, query_count).astype(jnp.float32)
    slot_k = jnp.sum(picked * position[:, None, :].astype(jnp.float32), axis=2).reshape(slots, 1)
    occupied = jnp.sum(picked, axis=2).reshape(slots, 1) > 0
    offsets = raw - slot_k.astype(jnp.int32) * block_labels
    inside = (offsets >= 0) & (offsets < block_labels) & occupied
    local_positive = jnp.where(inside, offsets, -1).astype(jnp.int32)

    incoming = lax.all_to_all(
        outgoing.reshape(devices, local_clusters, CAP, width),
        AXES, split_axis=0, concat_axis=2, tiled=True,
    ).reshape(local_clusters, devices * CAP, width)
    incoming_pos = lax.all_to_all(
        local_positive.reshape(devices, local_clusters, CAP, positive_count),
        AXES, split_axis=0, concat_axis=2, tiled=True,
    ).reshape(local_clusters, devices * CAP, positive_count)

    scores = jnp.einsum(
        "cnd,jcd->cnj", incoming, label_weight, preferred_element_type=jnp.float32
    )
    labels = jnp.arange(block_labels, dtype=jnp.int32)
    target = jnp.zeros(scores.shape, jnp.bool_)
    for column in range(positive_count):
        target = target | (incoming_pos[..., column : column + 1] == labels)
    signal = (jax.nn.sigmoid(scores) - target.astype(jnp.float32)).astype(jnp.bfloat16)
    weight_grad = jnp.einsum("cnj,cnd->jcd", signal, incoming, preferred_element_type=jnp.float32)
    row_grads = jnp.einsum(
        "cnj,jcd->cnd", signal, label_weight, preferred_element_type=jnp.float32
    ).astype(jnp.bfloat16)
    returned = lax.all_to_all(
        row_grads.reshape(1, local_clusters, devices * CAP, width),
        AXES, split_axis=2, concat_axis=0, tiled=True,
    ).reshape(slots, width)
    query_grad = lax.dot_general(
        dispatch, returned, (((0,), (0,)), ((), ())), preferred_element_type=jnp.float32
    )
    return (query_grad, weight_grad)


def solution(mesh):
    in_specs = (
        P(AXES, None),
        P(),
        P(),
        P(AXES, None),
        P(AXES, None),
        P(None, AXES, None),
    )
    out_specs = (P(AXES, None), P(None, AXES, None))
    return jax.shard_map(
        on_device, mesh=mesh, in_specs=in_specs, out_specs=out_specs, check_vma=False
    )
```

time: 1150 us -> 1150 us (level)
  the two profiles are of different devices: /device:TPU:10 before, /device:TPU:2 now
where the time goes in v1:
time: 1150 us; the launch traced here: 1140 us
  waiting for transfers between devices  713 us (62%)
  local copies, waits for them, and re-layouts  266 us (23%)
  matrix products  75.3 us (7%)
  other arithmetic  52.7 us (5%)
  starting transfers between devices  31.7 us (3%)
    all_to_all x1, waiting for transfers between devices, on_device(): lax.all_to_all(outgoing.reshape(devices, local_clusters, CAP, width), AXE...  372 us
    all_to_all x1, waiting for transfers between devices, on_device(): lax.all_to_all(row_grads.reshape(1, local_clusters, devices * CAP, width)...  341 us
    reshape x1, local copies, waits for them, and re-layouts, on_device(): incoming = lax.all_to_all(outgoing.reshape(devices, local_clusters, CAP,...  30.3 us
    reshape x1, local copies, waits for them, and re-layouts, on_device(): returned = lax.all_to_all(row_grads.reshape(1, local_clusters, devices *...  30.3 us
    reshape x1, local copies, waits for them, and re-layouts, on_device(): outgoing.reshape(devices, local_clusters, CAP, width)  30 us
    and x3, local copies, waits for them, and re-layouts, on_device(): dispatch = member[:, None, :] & (rank[:, None, :] == slot_of[None, :, None])  28.2 us
    eq x4, local copies, waits for them, and re-layouts, on_device(): dispatch = member[:, None, :] & (rank[:, None, :] == slot_of[None, :, None])  25.4 us
    all_to_all x2, local copies, waits for them, and re-layouts, on_device(): lax.all_to_all(row_grads.reshape(1, local_clusters, devices * CAP, width)...  24.6 us
  transfers between devices with their start and end apart: 3, of which 2 were waited for; matrix products, arithmetic and copies ran while one was open for 10% of the time, Pallas kernels for 0%

profile of v1, /device:TPU:2, one launch (start us, length us, event | category | flops | bytes accessed | tf_op | source)
XLA Modules:
  0.0 1140.1 jit_solution(16477713626988314673)
XLA Ops:
  0.6 0.0 copy-start
  0.6 5.9 fusion
  6.5 0.0 copy-start.4
  6.5 6.9 select_reduce_fusion
  13.5 0.8 fusion.13
  14.2 1.4 copy-done.2
  15.7 7.2 eq.169
  22.9 17.6 %eq.172 = f32[9216,384]{1,0:T(8,128)} reshape(f32[1536,6,384]{2,1,0:T(8,128)} %eq.169) | data formatting | bytes 28311552 | tf_op jit(solution)/shard_map/eq | solution.py:40
  40.5 7.6 and.43
  48.1 10.3 and.46
  58.4 0.1 eq.173
  58.5 0.5 eq.174
  59.0 0.0 copy-start.3
  59.1 2.0 convert_element_type.49
  61.0 0.0 copy-done.4
  61.1 0.4 copy-done.3
  61.4 13.0 %convert_reduce_fusion = (f32[1536,6]{1,0:T(8,128)}, f32[1536,6]{1,0:T(8,128)S(1)}) fusion(f32[1536,384]{1,0:T(8,128)S(1)} %copy-done.3, pred[1536,384]{1,0:T(8,128)(4,1)S(1)} %fusion, f32[1536,384]{1,0:T(8,128)S(1)} %convert_element_type.49), kind=kLoop, calls=%fused_computation.4 | loop fusion | flops 24754176 | bytes 5382144 | tf_op jit(solution)/shard_map/reduce_sum | solution.py:49
  74.4 0.1 convert_multiply_fusion.1
  74.5 0.5 mul.58
  75.0 1.2 broadcast_compare_fusion
  76.3 0.7 gt.16
  76.9 8.3 compare_and_fusion
  85.3 0.0 copy-start.6
  85.3 1.8 copy-done.6
  87.1 1.9 fusion.18
  89.0 0.1 and_select_fusion
  89.2 7.0 reshape.107
  96.2 9.8 copy.41
  106.0 4.2 reshape.111
  110.2 10.5 all-to-all-start.1
  120.8 1.1 fusion.26
  121.8 0.3 multiply_reduce_fusion
  122.1 15.4 %convolution_convert_fusion = bf16[9216,1024]{1,0:T(8,128)(2,1)} fusion(pred[9216,384]{1,0:T(32,128)(4,1)} %copy-done.6, f32[384,1024]{1,0:T(8,128)S(1)} %get-tuple-element.23, f32[1024]{0:T(1024)S(1)} %copy-done.9, f32[384]{0:T(512)S(1)} %add_rsqrt_fusion, f32[384]{0:T(512)S(1)} %broadcast_multiply_fusion), kind=kOutput, calls=%fused_computation.10 | convolution fusion | flops 7258767360 | bytes 23993344 | tf_op jit(solution)/shard_map/dot_general | solution.py:43
  137.5 30.0 %reshape.105 = bf16[128,12,6,1024]{3,2,1,0:T(8,128)(2,1)} reshape(bf16[9216,1024]{1,0:T(8,128)(2,1)} %convolution_convert_fusion) | data formatting | bytes 37748736 | tf_op jit(solution)/shard_map/reshape | solution.py:55
  167.6 0.0 all-to-all-done.1
  167.6 10.6 all-to-all-start
  178.1 0.5 broadcast.92
  178.6 1.4 reduce
  180.1 3.5 reshape.112
  183.6 12.4 %fusion.25 = (s32[12,768,1]{0,2,1:T(1,128)S(1)}, s32[12,768,1]{0,2,1:T(1,128)S(1)}, s32[12,768,1]{0,2,1:T(1,128)S(1)}, s32[12,768,1]{0,2,1:T(1,128)S(1)}, s32[12...) fusion(s32[12,768,8]{0,2,1:T(8,128)} %bitcast.45), kind=kLoop, calls=%fused_computation.60 | loop fusion | bytes 589824 | tf_op jit(solution)/shard_map/slice | solution.py:69
  196.0 0.1 copy.42
  196.1 0.2 copy.43
  196.3 0.2 copy.44
  196.4 0.2 copy.45
  196.6 0.2 copy.46
  196.8 0.2 copy.47
  196.9 0.2 copy.48
  197.1 0.2 copy.49
  197.3 371.9 %all-to-all-done = bf16[128,12,6,1024]{3,2,1,0:T(8,128)(2,1)} async-done(((bf16[128,12,6,1024]{3,2,1,0:T(8,128)(2,1)}), bf16[128,12,6,1024]{3,2,1,0:T(8,128)(2,1)}, u32[]{:S(2)}, u32[]{:S(2)}) %all-to-all-start) | async-done | bytes 18874400 | tf_op jit(solution)/shard_map/all_to_all | solution.py:54
  569.2 20.6 %copy.40 = bf16[1,12,128,6,1024]{4,3,2,1,0:T(8,128)(2,1)} copy(bf16[1,12,128,6,1024]{4,3,1,2,0:T(8,128)(2,1)} %bitcast.2) | data formatting | bytes 37748736 | tf_op jit(solution)/shard_map/all_to_all | solution.py:54
  589.8 30.3 %reshape.106 = bf16[12,768,1024]{2,1,0:T(8,128)(2,1)} reshape(bf16[1,12,128,6,1024]{4,3,2,1,0:T(8,128)(2,1)} %copy.40) | data formatting | bytes 37748736 | tf_op jit(solution)/shard_map/reshape | solution.py:57
  620.1 16.6 %subtract_convert_fusion = bf16[12,768,256]{2,1,0:T(8,128)(2,1)} fusion(s32[12,768]{1,0:T(8,128)S(1)} %copy.49, s32[12,768]{1,0:T(8,128)S(1)} %copy.48, s32[12,768]{1,0:T(8,128)S(1)} %copy.47, s32[12,768]{1,0:T(8,128)S(1)} %copy.46, s32[12,768]{1,0:T(8,128)S(1)} %copy.45, s32[12,768]{1,0:T(8,128)S(1)} %copy.44, s32[12,768]{1,0:T(8,128)S(1)} %copy.43, ...), kind=kOutput, calls=%fused_computation.12 | convolution fusion | flops 4881383424 | bytes 30179328 | tf_op jit(solution)/shard_map/cnd,jcd->cnj/dot_general | solution.py:63
  636.7 12.5 %convert_bitcast_fusion = bf16[1,12,768,1024]{3,2,1,0:T(8,128)(2,1)} fusion(bf16[12,768,256]{2,1,0:T(8,128)(2,1)} %subtract_convert_fusion, bf16[256,12,1024]{2,0,1:T(8,128)(2,1)} %param.11), kind=kOutput, calls=%fused_computation.7 | convolution fusion | flops 4841275392 | bytes 29884416 | tf_op jit(solution)/shard_map/cnj,jcd->cnd/dot_general | solution.py:72
  649.2 20.3 %copy.50 = bf16[1,12,768,1024]{3,1,0,2:T(8,128)(2,1)} copy(bf16[1,12,768,1024]{3,2,1,0:T(8,128)(2,1)} %convert_bitcast_fusion) | data formatting | bytes 37748736 | tf_op jit(solution)/shard_map/reshape | solution.py:76
  669.5 10.6 all-to-all-start.2
  680.1 13.4 %fusion.2 = pred[1536,6,384]{2,1,0:T(8,128)(4,1)} fusion(f32[1536,384]{1,0:T(8,128)} %copy-done.2, pred[1536,384]{1,0:T(8,128)(4,1)S(1)} %copy-done.5), kind=kLoop, calls=%fused_computation.9 | loop fusion | flops 7077888 | bytes 6488064 | tf_op jit(solution)/shard_map/and | solution.py:40
  693.5 10.3 and.45
  703.8 13.6 %convolution_bitcast_fusion = f32[256,12,1024]{0,2,1:T(8,128)} fusion(bf16[12,768,1024]{2,1,0:T(8,128)(2,1)} %reshape.106, bf16[12,768,256]{2,1,0:T(8,128)(2,1)} %subtract_convert_fusion), kind=kOutput, calls=%fused_computation.28 | convolution fusion | flops 4831838208 | bytes 36175872 | tf_op jit(solution)/shard_map/cnj,cnd->jcd/dot_general | solution.py:71
  717.4 12.6 %copy.54 = f32[256,12,1024]{2,0,1:T(8,128)} copy(f32[256,12,1024]{0,2,1:T(8,128)} %convolution_bitcast_fusion) | data formatting | bytes 25165824
  730.0 341.2 %all-to-all-done.2 = bf16[1,12,768,1024]{3,1,0,2:T(8,128)(2,1)} async-done(((bf16[1,12,768,1024]{3,1,0,2:T(8,128)(2,1)}), bf16[1,12,768,1024]{3,1,0,2:T(8,128)(2,1)}, u32[]{:S(2)}, u32[]{:S(2)}) %all-to-all-start.2) | async-done | bytes 18874400 | tf_op jit(solution)/shard_map/all_to_all | solution.py:75
  1071.2 16.1 %copy.58 = bf16[1,12,128,6,1024]{4,3,2,1,0:T(8,128)(2,1)S(1)} copy(bf16[1,12,128,6,1024]{4,1,3,2,0:T(8,128)(2,1)} %bitcast.17) | data formatting | bytes 37748736 | tf_op jit(solution)/shard_map/all_to_all | solution.py:75
  1087.3 8.6 copy.52
  1095.8 30.3 %reshape.110 = bf16[9216,1024]{1,0:T(8,128)(2,1)} reshape(bf16[128,1,12,6,1024]{4,3,2,0,1:T(8,128)(2,1)} %copy.52) | data formatting | bytes 37748736 | tf_op jit(solution)/shard_map/reshape | solution.py:78
  1126.1 13.5 %fusion.27 = f32[384,1024]{1,0:T(8,128)} fusion(pred[9216,384]{1,0:T(32,128)(4,1)} %and.45, bf16[9216,1024]{1,0:T(8,128)(2,1)} %reshape.110), kind=kOutput, calls=%fused_computation.62 | convolution fusion | flops 7247757312 | bytes 23986176 | tf_op jit(solution)/shard_map/dot_general | solution.py:79
  (15 shorter events, 0.1 us)
Async XLA Ops:
  0.6 120.1 %copy-start = (bf16[1024,1024]{1,0:T(8,128)(2,1)S(1)}, bf16[1024,1024]{1,0:T(8,128)(2,1)}, u32[]{:S(2)}) copy-start(bf16[1024,1024]{1,0:T(8,128)(2,1)} %param.7) | copy-start | bytes 6291460
  6.5 54.5 %copy-start.4 = (pred[1536,384]{1,0:T(8,128)(4,1)}, pred[1536,384]{1,0:T(8,128)(4,1)S(1)}, u32[]{:S(2)}) copy-start(pred[1536,384]{1,0:T(8,128)(4,1)S(1)} %fusion) | copy-start | bytes 1769476
  14.2 1.5 copy-start.2
  48.1 10.9 copy-start.7
  59.0 2.4 copy-start.3
  85.3 1.8 copy-start.6
  96.2 24.6 %copy-start.8 = (bf16[384,1024]{1,0:T(8,128)(2,1)S(1)}, bf16[384,1024]{1,0:T(8,128)(2,1)}, u32[]{:S(2)}) copy-start(bf16[384,1024]{1,0:T(8,128)(2,1)} %param.6) | copy-start | bytes 2359300
  106.0 16.2 %copy-start.9 = (f32[1024]{0:T(1024)S(1)}, f32[1024]{0:T(1024)}, u32[]{:S(2)}) copy-start(f32[1024]{0:T(1024)} %param.8) | copy-start | bytes 12292
  110.2 57.4 %all-to-all-start.1 = ((s32[128,1,576]{2,1,0:T(1,128)}), s32[128,1,576]{2,1,0:T(1,128)S(1)}, u32[]{:S(2)}, u32[]{:S(2)}) async-start(s32[128,1,576]{2,1,0:T(1,128)} %reshape.111), calls=%async_computation.1 | async-start | bytes 655360 | tf_op jit(solution)/shard_map/all_to_all | solution.py:58
  167.6 401.6 %all-to-all-start = ((bf16[128,12,6,1024]{3,2,1,0:T(8,128)(2,1)}), bf16[128,12,6,1024]{3,2,1,0:T(8,128)(2,1)}, u32[]{:S(2)}, u32[]{:S(2)}) async-start(bf16[128,12,6,1024]{3,2,1,0:T(8,128)(2,1)} %reshape.105), calls=%async_computation | async-start | bytes 50331648 | tf_op jit(solution)/shard_map/all_to_all | solution.py:54
  669.5 10.6 copy-start.5
  669.5 401.7 %all-to-all-start.2 = ((bf16[1,12,768,1024]{3,1,0,2:T(8,128)(2,1)}), bf16[1,12,768,1024]{3,1,0,2:T(8,128)(2,1)}, u32[]{:S(2)}, u32[]{:S(2)}) async-start(bf16[1,12,768,1024]{3,1,0,2:T(8,128)(2,1)} %copy.50), calls=%async_computation.2 | async-start | bytes 50331648 | tf_op jit(solution)/shard_map/all_to_all | solution.py:75
  1126.1 13.5 %copy-start.1 = (bf16[1024,1024]{1,0:T(8,128)(2,1)S(1)}, bf16[1024,1024]{1,0:T(8,128)(2,1)}, u32[]{:S(2)}) copy-start(bf16[1024,1024]{1,0:T(8,128)(2,1)} %param.7) | copy-start | bytes 6291460

commit v2 on v1

--- a/solution.py
+++ b/solution.py
@@ -26,39 +26,59 @@
     slots = clusters * CAP
 
     cluster_id = jnp.arange(clusters, dtype=jnp.int32)
-    hit = shortlist.T[:, None, :] == cluster_id[None, :, None]
-    member = jnp.any(hit, axis=0)
-    position = jnp.sum(
-        jnp.where(hit, jnp.arange(shortlist_size, dtype=jnp.int32)[:, None, None], 0), axis=0
-    )
+    member = jnp.any(shortlist.T[:, None, :] == cluster_id[None, :, None], axis=0)
     earlier = (
         jnp.arange(query_count, dtype=jnp.int32)[:, None]
         < jnp.arange(query_count, dtype=jnp.int32)[None, :]
     ).astype(jnp.bfloat16)
     rank = jnp.dot(member.astype(jnp.bfloat16), earlier, preferred_element_type=jnp.float32)
-    slot_of = jnp.arange(CAP, dtype=jnp.float32)
-    dispatch = member[:, None, :] & (rank[:, None, :] == slot_of[None, :, None])
-    dispatch = dispatch.astype(jnp.bfloat16).reshape(slots, query_count)
+    level = jnp.where(member, rank, float(CAP + 1)).astype(jnp.bfloat16)
+    slot_rank = (jnp.arange(slots, dtype=jnp.int32) % CAP).astype(jnp.bfloat16)
+    dispatch = (jnp.repeat(level, CAP, axis=0) == slot_rank[:, None]).astype(jnp.bfloat16)
 
     outgoing = jnp.dot(dispatch, queries, preferred_element_type=jnp.float32).astype(jnp.bfloat16)
-    split = jnp.concatenate([positives // 256, positives % 256], axis=1).astype(jnp.bfloat16)
-    gathered = jnp.dot(dispatch, split, preferred_element_type=jnp.float32)
-    raw = (gathered[:, :positive_count] * 256 + gathered[:, positive_count:]).astype(jnp.int32)
-    picked = dispatch.reshape(clusters, CAP, query_count).astype(jnp.float32)
-    slot_k = jnp.sum(picked * position[:, None, :].astype(jnp.float32), axis=2).reshape(slots, 1)
-    occupied = jnp.sum(picked, axis=2).reshape(slots, 1) > 0
-    offsets = raw - slot_k.astype(jnp.int32) * block_labels
+    parts = jnp.concatenate(
+        [shortlist // 256, shortlist % 256, positives // 256, positives % 256,
+         jnp.ones((query_count, 1), jnp.int32)],
+        axis=1,
+    ).astype(jnp.bfloat16)
+    gathered = jnp.dot(dispatch, parts, preferred_element_type=jnp.float32)
+    k_hi = gathered[:, :shortlist_size]
+    k_lo = gathered[:, shortlist_size : 2 * shortlist_size]
+    p_base = 2 * shortlist_size
+    slot_list = (k_hi * 256 + k_lo).astype(jnp.int32)
+    raw = (
+        gathered[:, p_base : p_base + positive_count] * 256
+        + gathered[:, p_base + positive_count : p_base + 2 * positive_count]
+    ).astype(jnp.int32)
+    occupied = gathered[:, p_base + 2 * positive_count :] > 0.5
+    slot_cluster = jnp.arange(slots, dtype=jnp.int32)[:, None] // CAP
+    slot_k = jnp.sum(
+        jnp.where(slot_list == slot_cluster, jnp.arange(shortlist_size, dtype=jnp.int32), 0),
+        axis=1, keepdims=True,
+    )
+    offsets = raw - slot_k * block_labels
     inside = (offsets >= 0) & (offsets < block_labels) & occupied
     local_positive = jnp.where(inside, offsets, -1).astype(jnp.int32)
 
+    per_dst = local_clusters * CAP
     incoming = lax.all_to_all(
-        outgoing.reshape(devices, local_clusters, CAP, width),
-        AXES, split_axis=0, concat_axis=2, tiled=True,
-    ).reshape(local_clusters, devices * CAP, width)
+        outgoing.reshape(devices, per_dst, width), AXES, split_axis=0, concat_axis=0, tiled=True
+    )
+    incoming = (
+        incoming.reshape(devices, local_clusters, CAP, width)
+        .transpose(1, 0, 2, 3)
+        .reshape(local_clusters, devices * CAP, width)
+    )
     incoming_pos = lax.all_to_all(
-        local_positive.reshape(devices, local_clusters, CAP, positive_count),
-        AXES, split_axis=0, concat_axis=2, tiled=True,
-    ).reshape(local_clusters, devices * CAP, positive_count)
+        local_positive.reshape(devices, per_dst, positive_count),
+        AXES, split_axis=0, concat_axis=0, tiled=True,
+    )
+    incoming_pos = (
+        incoming_pos.reshape(devices, local_clusters, CAP, positive_count)
+        .transpose(1, 0, 2, 3)
+        .reshape(local_clusters, devices * CAP, positive_count)
+    )
 
     scores = jnp.einsum(
         "cnd,jcd->cnj", incoming, label_weight, preferred_element_type=jnp.float32
@@ -72,9 +92,13 @@
     row_grads = jnp.einsum(
         "cnj,jcd->cnd", signal, label_weight, preferred_element_type=jnp.float32
     ).astype(jnp.bfloat16)
+    row_grads = (
+        row_grads.reshape(local_clusters, devices, CAP, width)
+        .transpose(1, 0, 2, 3)
+        .reshape(devices, per_dst, width)
+    )
     returned = lax.all_to_all(
-        row_grads.reshape(1, local_clusters, devices * CAP, width),
-        AXES, split_axis=2, concat_axis=0, tiled=True,
+        row_grads, AXES, split_axis=0, concat_axis=0, tiled=True
     ).reshape(slots, width)
     query_grad = lax.dot_general(
         dispatch, returned, (((0,), (0,)), ((), ())), preferred_element_type=jnp.float32

time: 1150 us -> 822 us (0.71)
  the two profiles are of different devices: /device:TPU:2 before, /device:TPU:10 now
where the time goes in v2:
time: 822 us; the launch traced here: 811 us
  waiting for transfers between devices  493 us (60%)
  local copies, waits for them, and re-layouts  187 us (23%)
  matrix products  84.4 us (10%)
  starting transfers between devices  28.7 us (3%)
  other arithmetic  16.8 us (2%)
    all_to_all x1, waiting for transfers between devices, on_device(): lax.all_to_all(outgoing.reshape(devices, per_dst, width), AXES, split_axi...  259 us
    all_to_all x1, waiting for transfers between devices, on_device(): lax.all_to_all(row_grads, AXES, split_axis=0, concat_axis=0, tiled=True)  234 us
    reshape x1, local copies, waits for them, and re-layouts, on_device(): incoming = incoming.reshape(devices, local_clusters, CAP, width).transpos...  30.3 us
    reshape x1, local copies, waits for them, and re-layouts, on_device(): row_grads.reshape(local_clusters, devices, CAP, width).transpose(1, 0, 2, 3)  30 us
    dot_general x1, matrix products, on_device(): jnp.dot(dispatch, queries, preferred_element_type=jnp.float32)  19.3 us
    transpose x1, local copies, waits for them, and re-layouts, on_device(): row_grads = row_grads.reshape(local_clusters, devices, CAP, width).transp...  17.5 us
    all_to_all x1, local copies, waits for them, and re-layouts, on_device(): lax.all_to_all(outgoing.reshape(devices, per_dst, width), AXES, split_axi...  17.4 us
    dot_general x1, matrix products, on_device(): jnp.einsum('cnd,jcd->cnj', incoming, label_weight, preferred_element_type...  16.5 us
  transfers between devices with their start and end apart: 3, of which 2 were waited for; matrix products, arithmetic and copies ran while one was open for 10% of the time, Pallas kernels for 0%

profile of v2, /device:TPU:10, one launch (start us, length us, event | category | flops | bytes accessed | tf_op | source)
XLA Modules:
  0.0 811.5 jit_solution(10877003999540765056)
XLA Ops:
  0.6 0.0 copy-start
  0.7 0.9 fusion.35
  1.6 5.7 fusion
  7.3 0.8 fusion.13
  8.1 0.0 copy-start.2
  8.1 1.0 copy-done.2
  9.1 8.6 %broadcast_in_dim.21 = bf16[1536,6,384]{2,1,0:T(8,128)(2,1)} broadcast(bf16[1536,384]{1,0:T(8,128)(2,1)S(1)} %fusion.13), dimensions={0,2} | broadcast | bytes 8257536 | tf_op jit(solution)/shard_map/broadcast_in_dim | solution.py:37
  17.7 0.0 copy-start.5
  17.7 0.0 copy-start.6
  17.7 12.7 %reshape.114 = bf16[9216,384]{1,0:T(8,128)(2,1)} reshape(bf16[1536,6,384]{2,1,0:T(8,128)(2,1)} %broadcast_in_dim.21) | data formatting | bytes 14155776 | tf_op jit(solution)/shard_map/reshape | solution.py:37
  30.4 0.0 copy-done.5
  30.4 0.0 copy-done.6
  30.5 6.2 fusion.8
  36.7 0.0 copy-start.7
  36.7 0.1 compare_reduce_fusion
  36.8 0.2 select_reduce_fusion
  37.1 0.1 and_select_fusion
  37.2 0.5 reshape.118
  37.7 1.1 copy.62
  38.8 10.7 %all-to-all-start.1 = ((s32[128,72,8]{1,2,0:T(8,128)}), s32[128,72,8]{1,2,0:T(8,128)S(1)}, u32[]{:S(2)}, u32[]{:S(2)}) async-start(s32[128,72,8]{1,2,0:T(8,128)} %copy.62), calls=%async_computation.1 | async-start | bytes 1048576 | tf_op jit(solution)/shard_map/all_to_all | solution.py:73
  49.5 0.0 copy-done
  49.5 2.2 fusion.42
  51.7 0.0 copy-start.4
  51.7 1.1 copy-done.4
  52.9 0.3 multiply_reduce_fusion
  53.2 0.0 copy-done.7
  53.2 19.3 %convolution_convert_fusion = bf16[9216,1024]{1,0:T(8,128)(2,1)} fusion(bf16[9216,384]{1,0:T(8,128)(2,1)} %reshape.114, bf16[9216]{0:T(1024)(128)(2,1)S(1)} %fusion.25, f32[384,1024]{1,0:T(8,128)} %copy-done.4, f32[1024]{0:T(1024)S(1)} %copy-done.7, f32[384]{0:T(512)S(1)} %add_rsqrt_fusion, f32[384]{0:T(512)S(1)} %broadcast_multiply_fusion.1), kind=kOutput, calls=%fused_computation.2 | convolution fusion | flops 7262306304 | bytes 27550720 | tf_op jit(solution)/shard_map/dot_general | solution.py:39
  72.5 0.0 all-to-all-done.1
  72.5 10.6 %all-to-all-start = ((bf16[128,72,1024]{2,1,0:T(8,128)(2,1)}), bf16[128,72,1024]{2,1,0:T(8,128)(2,1)}, u32[]{:S(2)}, u32[]{:S(2)}) async-start(bf16[128,72,1024]{2,1,0:T(8,128)(2,1)} %bitcast.39), calls=%async_computation | async-start | bytes 37748736 | tf_op jit(solution)/shard_map/all_to_all | solution.py:65
  83.1 0.2 copy.63
  83.3 2.2 copy.64
  85.5 12.9 %fusion.41 = (s32[12,768,1]{0,2,1:T(1,128)S(1)}, s32[12,768,1]{0,2,1:T(1,128)S(1)}, s32[12,768,1]{0,2,1:T(1,128)S(1)}, s32[12,768,1]{0,2,1:T(1,128)S(1)}, s32[12...) fusion(s32[12,768,8]{0,2,1:T(8,128)} %bitcast.40), kind=kLoop, calls=%fused_computation.91 | loop fusion | bytes 589824 | tf_op jit(solution)/shard_map/slice | solution.py:89
  98.5 0.1 copy.65
  98.6 0.2 copy.66
  98.8 0.2 copy.67
  98.9 0.2 copy.68
  99.1 0.2 copy.69
  99.3 0.2 copy.70
  99.4 0.2 copy.71
  99.6 0.2 copy.72
  99.7 259.1 %all-to-all-done = bf16[128,72,1024]{2,1,0:T(8,128)(2,1)} async-done(((bf16[128,72,1024]{2,1,0:T(8,128)(2,1)}), bf16[128,72,1024]{2,1,0:T(8,128)(2,1)}, u32[]{:S(2)}, u32[]{:S(2)}) %all-to-all-start) | async-done | bytes 18874400 | tf_op jit(solution)/shard_map/all_to_all | solution.py:65
  358.8 17.4 %copy.60 = bf16[128,72,1024]{2,0,1:T(8,128)(2,1)S(1)} copy(bf16[128,72,1024]{2,1,0:T(8,128)(2,1)} %all-to-all-done) | data formatting | bytes 37748736 | tf_op jit(solution)/shard_map/all_to_all | solution.py:65
  376.2 15.3 %copy.61 = bf16[12,128,6,1024]{3,2,1,0:T(8,128)(2,1)} copy(bf16[12,128,6,1024]{3,1,2,0:T(8,128)(2,1)S(1)} %bitcast.37) | data formatting | bytes 37748736 | tf_op jit(solution)/shard_map/transpose | solution.py:70
  391.6 30.3 %reshape.117 = bf16[12,768,1024]{2,1,0:T(8,128)(2,1)} reshape(bf16[12,128,6,1024]{3,2,1,0:T(8,128)(2,1)} %copy.61) | data formatting | bytes 37748736 | tf_op jit(solution)/shard_map/reshape | solution.py:71
  421.9 16.5 %subtract_convert_fusion = bf16[12,768,256]{2,1,0:T(8,128)(2,1)} fusion(s32[12,768]{1,0:T(8,128)S(1)} %copy.72, s32[12,768]{1,0:T(8,128)S(1)} %copy.71, s32[12,768]{1,0:T(8,128)S(1)} %copy.70, s32[12,768]{1,0:T(8,128)S(1)} %copy.69, s32[12,768]{1,0:T(8,128)S(1)} %copy.68, s32[12,768]{1,0:T(8,128)S(1)} %copy.67, s32[12,768]{1,0:T(8,128)S(1)} %copy.66, ...), kind=kOutput, calls=%fused_computation.4 | convolution fusion | flops 4881383424 | bytes 30179328 | tf_op jit(solution)/shard_map/cnd,jcd->cnj/dot_general | solution.py:83
  438.4 12.5 %convolution_convert_fusion.1 = bf16[12,768,1024]{2,1,0:T(8,128)(2,1)} fusion(bf16[12,768,256]{2,1,0:T(8,128)(2,1)} %subtract_convert_fusion, bf16[256,12,1024]{2,0,1:T(8,128)(2,1)} %param.11), kind=kOutput, calls=%fused_computation.3 | convolution fusion | flops 4841275392 | bytes 29884416 | tf_op jit(solution)/shard_map/cnj,jcd->cnd/dot_general | solution.py:92
  450.9 30.0 %reshape.121 = bf16[12,128,6,1024]{3,2,1,0:T(8,128)(2,1)} reshape(bf16[12,768,1024]{2,1,0:T(8,128)(2,1)} %convolution_convert_fusion.1) | data formatting | bytes 37748736 | tf_op jit(solution)/shard_map/reshape | solution.py:96
  481.0 17.5 %copy.73 = bf16[128,12,6,1024]{3,0,2,1:T(8,128)(2,1)S(1)} copy(bf16[128,12,6,1024]{3,2,0,1:T(8,128)(2,1)} %bitcast.36) | data formatting | bytes 37748736 | tf_op jit(solution)/shard_map/transpose | solution.py:97
  498.5 12.2 %copy.74 = bf16[128,72,1024]{2,1,0:T(8,128)(2,1)} copy(bf16[128,72,1024]{2,0,1:T(8,128)(2,1)S(1)} %bitcast.38) | data formatting | bytes 37748736 | tf_op jit(solution)/shard_map/reshape | solution.py:98
  510.6 0.0 copy-start.3
  510.6 7.4 all-to-all-start.2
  518.1 0.5 fusion.14
  518.6 0.0 copy-done.3
  518.6 8.8 %broadcast_compare_fusion = pred[1536,6,384]{2,1,0:T(8,128)(4,1)} fusion(bf16[1536,6]{1,0:T(8,128)(2,1)S(1)} %fusion.14, bf16[1536,384]{1,0:T(8,128)(2,1)S(1)} %copy-done.3), kind=kLoop, calls=%fused_computation.20 | loop fusion | flops 3538944 | bytes 4737024 | tf_op jit(solution)/shard_map/eq | solution.py:37
  527.4 10.3 %eq.173 = pred[9216,384]{1,0:T(32,128)(4,1)} reshape(pred[1536,6,384]{2,1,0:T(8,128)(4,1)} %broadcast_compare_fusion) | data formatting | bytes 7077888 | tf_op jit(solution)/shard_map/eq | solution.py:37
  537.7 13.4 %convolution_bitcast_fusion = f32[256,12,1024]{0,2,1:T(8,128)} fusion(bf16[12,768,1024]{2,1,0:T(8,128)(2,1)} %reshape.117, bf16[12,768,256]{2,1,0:T(8,128)(2,1)} %subtract_convert_fusion), kind=kOutput, calls=%fused_computation.21 | convolution fusion | flops 4831838208 | bytes 36175872 | tf_op jit(solution)/shard_map/cnj,cnd->jcd/dot_general | solution.py:91
  551.1 12.6 %copy.76 = f32[256,12,1024]{2,0,1:T(8,128)} copy(f32[256,12,1024]{0,2,1:T(8,128)} %convolution_bitcast_fusion) | data formatting | bytes 25165824
  563.7 233.8 %all-to-all-done.2 = bf16[128,72,1024]{2,1,0:T(8,128)(2,1)} async-done(((bf16[128,72,1024]{2,1,0:T(8,128)(2,1)}), bf16[128,72,1024]{2,1,0:T(8,128)(2,1)}, u32[]{:S(2)}, u32[]{:S(2)}) %all-to-all-start.2) | async-done | bytes 18874400 | tf_op jit(solution)/shard_map/all_to_all | solution.py:100
  797.6 0.0 copy-start.1
  797.6 13.4 %fusion.43 = f32[384,1024]{1,0:T(8,128)} fusion(pred[9216,384]{1,0:T(32,128)(4,1)} %eq.173, bf16[9216,1024]{1,0:T(8,128)(2,1)} %bitcast.17), kind=kOutput, calls=%fused_computation.93 | convolution fusion | flops 7247757312 | bytes 23986176 | tf_op jit(solution)/shard_map/dot_general | solution.py:103
  811.0 0.0 copy-done.1
  (9 shorter events, 0.1 us)
Async XLA Ops:
  0.6 48.9 %copy-start = (bf16[1024,1024]{1,0:T(8,128)(2,1)S(1)}, bf16[1024,1024]{1,0:T(8,128)(2,1)}, u32[]{:S(2)}) copy-start(bf16[1024,1024]{1,0:T(8,128)(2,1)} %param.7) | copy-start | bytes 6291460
  8.1 1.0 copy-start.2
  17.7 12.7 %copy-start.5 = (s32[384,16]{0,1:T(8,128)S(1)}, s32[384,16]{0,1:T(8,128)}, u32[]{:S(2)}) copy-start(s32[384,16]{0,1:T(8,128)} %param.9) | copy-start | bytes 73732
  17.7 12.7 %copy-start.6 = (s32[384,8]{0,1:T(8,128)S(1)}, s32[384,8]{0,1:T(8,128)}, u32[]{:S(2)}) copy-start(s32[384,8]{0,1:T(8,128)} %param.10) | copy-start | bytes 36868
  36.7 16.5 %copy-start.7 = (f32[1024]{0:T(1024)S(1)}, f32[1024]{0:T(1024)}, u32[]{:S(2)}) copy-start(f32[1024]{0:T(1024)} %param.8) | copy-start | bytes 12292
  38.8 33.7 %all-to-all-start.1 = ((s32[128,72,8]{1,2,0:T(8,128)}), s32[128,72,8]{1,2,0:T(8,128)S(1)}, u32[]{:S(2)}, u32[]{:S(2)}) async-start(s32[128,72,8]{1,2,0:T(8,128)} %copy.62), calls=%async_computation.1 | async-start | bytes 1048576 | tf_op jit(solution)/shard_map/all_to_all | solution.py:73
  51.7 1.1 copy-start.4
  72.5 286.3 %all-to-all-start = ((bf16[128,72,1024]{2,1,0:T(8,128)(2,1)}), bf16[128,72,1024]{2,1,0:T(8,128)(2,1)}, u32[]{:S(2)}, u32[]{:S(2)}) async-start(bf16[128,72,1024]{2,1,0:T(8,128)(2,1)} %bitcast.39), calls=%async_computation | async-start | bytes 37748736 | tf_op jit(solution)/shard_map/all_to_all | solution.py:65
  510.6 7.9 copy-start.3
  510.6 286.9 %all-to-all-start.2 = ((bf16[128,72,1024]{2,1,0:T(8,128)(2,1)}), bf16[128,72,1024]{2,1,0:T(8,128)(2,1)}, u32[]{:S(2)}, u32[]{:S(2)}) async-start(bf16[128,72,1024]{2,1,0:T(8,128)(2,1)} %copy.74), calls=%async_computation.2 | async-start | bytes 37748736 | tf_op jit(solution)/shard_map/all_to_all | solution.py:100
  797.6 13.4 %copy-start.1 = (bf16[1024,1024]{1,0:T(8,128)(2,1)S(1)}, bf16[1024,1024]{1,0:T(8,128)(2,1)}, u32[]{:S(2)}) copy-start(bf16[1024,1024]{1,0:T(8,128)(2,1)} %param.7) | copy-start | bytes 6291460

commit v3 on v2

v3 whole, which is shorter than its diff:
```python
import jax
import jax.numpy as jnp
from jax import lax
from jax.sharding import PartitionSpec as P
from jax.experimental import pallas as pl
from jax.experimental.pallas import tpu as pltpu

CAP = 6
AXES = ("row", "col")


def encode(pooled, enc_weight, norm_gain):
    projected = jnp.dot(pooled, enc_weight, preferred_element_type=jnp.float32)
    average = jnp.mean(projected, axis=-1, keepdims=True)
    centred = projected - average
    spread = jnp.mean(centred * centred, axis=-1, keepdims=True)
    return (centred * lax.rsqrt(spread + 1e-05) * norm_gain).astype(jnp.bfloat16)


def cluster_kernel(incoming_ref, positive_ref, weight_ref, grad_ref, rows_ref):
    block = weight_ref[0]
    x = incoming_ref[...]
    scores = lax.dot_general(
        x, block, (((1,), (1,)), ((), ())), preferred_element_type=jnp.float32
    )
    labels = lax.broadcasted_iota(jnp.int32, (1, block.shape[0]), 1)
    marks = positive_ref[...]
    target = marks[:, 0:1] == labels
    for column in range(1, marks.shape[1]):
        target = target | (marks[:, column : column + 1] == labels)
    signal = (jax.nn.sigmoid(scores) - target.astype(jnp.float32)).astype(jnp.bfloat16)
    grad_ref[0] = lax.dot_general(
        signal, x, (((0,), (0,)), ((), ())), preferred_element_type=jnp.float32
    )
    rows_ref[...] = jnp.dot(signal, block, preferred_element_type=jnp.float32).astype(jnp.bfloat16)


def on_device(pooled, enc_weight, norm_gain, shortlist, positives, label_weight):
    queries = encode(pooled, enc_weight, norm_gain)
    devices = lax.axis_size("row") * lax.axis_size("col")
    query_count, width = queries.shape
    block_labels, local_clusters, _ = label_weight.shape
    shortlist_size = shortlist.shape[1]
    positive_count = positives.shape[1]
    clusters = devices * local_clusters
    slots = clusters * CAP
    per_dst = local_clusters * CAP

    local_of = jnp.arange(local_clusters, dtype=jnp.int32)[:, None]
    device_of = jnp.arange(devices, dtype=jnp.int32)[None, :]
    cluster_id = (device_of * local_clusters + local_of).reshape(clusters)
    member = jnp.any(shortlist.T[:, None, :] == cluster_id[None, :, None], axis=0)
    earlier = (
        jnp.arange(query_count, dtype=jnp.int32)[:, None]
        < jnp.arange(query_count, dtype=jnp.int32)[None, :]
    ).astype(jnp.bfloat16)
    rank = jnp.dot(member.astype(jnp.bfloat16), earlier, preferred_element_type=jnp.float32)
    level = jnp.where(member, rank, float(CAP + 1)).astype(jnp.bfloat16)
    level = level.reshape(local_clusters, 1, devices, query_count)
    slot_rank = jnp.arange(CAP, dtype=jnp.int32).astype(jnp.bfloat16)[None, :, None, None]
    dispatch = (level == slot_rank).astype(jnp.bfloat16).reshape(slots, query_count)

    outgoing = jnp.dot(dispatch, queries, preferred_element_type=jnp.float32).astype(jnp.bfloat16)
    parts = jnp.concatenate(
        [shortlist // 256, shortlist % 256, positives // 256, positives % 256,
         jnp.ones((query_count, 1), jnp.int32)],
        axis=1,
    ).astype(jnp.bfloat16)
    gathered = jnp.dot(dispatch, parts, preferred_element_type=jnp.float32)
    k_hi = gathered[:, :shortlist_size]
    k_lo = gathered[:, shortlist_size : 2 * shortlist_size]
    p_base = 2 * shortlist_size
    slot_list = (k_hi * 256 + k_lo).astype(jnp.int32)
    raw = (
        gathered[:, p_base : p_base + positive_count] * 256
        + gathered[:, p_base + positive_count : p_base + 2 * positive_count]
    ).astype(jnp.int32)
    occupied = gathered[:, p_base + 2 * positive_count :] > 0.5
    row = jnp.arange(slots, dtype=jnp.int32)[:, None]
    slot_cluster = (row % devices) * local_clusters + row // (CAP * devices)
    slot_k = jnp.sum(
        jnp.where(slot_list == slot_cluster, jnp.arange(shortlist_size, dtype=jnp.int32), 0),
        axis=1, keepdims=True,
    )
    offsets = raw - slot_k * block_labels
    inside = (offsets >= 0) & (offsets < block_labels) & occupied
    local_positive = jnp.where(inside, offsets, -1).astype(jnp.int32)

    incoming = lax.all_to_all(
        outgoing.reshape(per_dst, devices, width), AXES, split_axis=1, concat_axis=1, tiled=True
    ).reshape(slots, width)
    incoming_pos = lax.all_to_all(
        local_positive.reshape(per_dst, devices, positive_count),
        AXES, split_axis=1, concat_axis=1, tiled=True,
    ).reshape(slots, positive_count)
    by_cluster = jnp.transpose(label_weight, (1, 0, 2))
    rows_per_cluster = CAP * devices
    grad, row_grads = pl.pallas_call(
        cluster_kernel,
        grid=(local_clusters,),
        in_specs=[
            pl.BlockSpec((rows_per_cluster, width), lambda c: (c, 0)),
            pl.BlockSpec((rows_per_cluster, positive_count), lambda c: (c, 0)),
            pl.BlockSpec((1, block_labels, width), lambda c: (c, 0, 0)),
        ],
        out_specs=[
            pl.BlockSpec((1, block_labels, width), lambda c: (c, 0, 0)),
            pl.BlockSpec((rows_per_cluster, width), lambda c: (c, 0)),
        ],
        out_shape=[
            jax.ShapeDtypeStruct((local_clusters, block_labels, width), jnp.float32),
            jax.ShapeDtypeStruct((slots, width), jnp.bfloat16),
        ],
        compiler_params=pltpu.CompilerParams(vmem_limit_bytes=48 * 1024 * 1024),
        cost_estimate=pl.CostEstimate(
            flops=6 * slots * block_labels * width,
            transcendentals=slots * block_labels,
            bytes_accessed=2 * slots * width * 2 + local_clusters * block_labels * width * 6,
        ),
    )(incoming, incoming_pos, by_cluster)
    weight_grad = jnp.transpose(grad, (1, 0, 2))
    returned = lax.all_to_all(
        row_grads.reshape(per_dst, devices, width), AXES, split_axis=1, concat_axis=1, tiled=True
    ).reshape(slots, width)
    query_grad = lax.dot_general(
        dispatch, returned, (((0,), (0,)), ((), ())), preferred_element_type=jnp.float32
    )
    return (query_grad, weight_grad)


def solution(mesh):
    in_specs = (
        P(AXES, None),
        P(),
        P(),
        P(AXES, None),
        P(AXES, None),
        P(None, AXES, None),
    )
    out_specs = (P(AXES, None), P(None, AXES, None))
    return jax.shard_map(
        on_device, mesh=mesh, in_specs=in_specs, out_specs=out_specs, check_vma=False
    )
```

time: 822 us -> 762 us (0.927); the launches traced: 811 us -> 760 us
  local copies, waits for them, and re-layouts: 187 us -> 91.3 us
  waiting for transfers between devices: 493 us -> 547 us
  matrix products: 84.4 us -> 33.5 us
  Pallas kernels: 0 us -> 40.1 us
    all_to_all x3, waiting for transfers between devices: 493 us -> 547 us  [the longest x1 275 us: on_device(): lax.all_to_all(row_grads.reshape(per_dst, devices, width), AXES, split_ax...]
    reshape x6 -> x3, local copies, waits for them, and re-layouts: 86.8 us -> 43.5 us  [the longest x1 20.8 us: on_device(): outgoing.reshape(per_dst, devices, width)]
    dot_general x3 -> x0, matrix products: 42.5 us -> none  [the longest x1 16.5 us: on_device(): jnp.einsum('cnd,jcd->cnj', incoming, label_weight, preferred_element_type...]
    pallas_call x0 -> x1, Pallas kernels: none -> 40.1 us  [on_device(): pl.pallas_call(cluster_kernel, grid=(local_clusters,), in_specs=[pl.Block...]
    transpose x3 -> x0, local copies, waits for them, and re-layouts: 35 us -> none  [the longest x1 17.5 us: on_device(): row_grads = row_grads.reshape(local_clusters, devices, CAP, width).transp...]
    all_to_all x2 -> x3, local copies, waits for them, and re-layouts: 17.6 us -> 47.6 us  [the longest x1 20.9 us: on_device(): lax.all_to_all(row_grads.reshape(per_dst, devices, width), AXES, split_ax...]
    unnamed x17 -> x16, local copies, waits for them, and re-layouts: 14.8 us -> 0.05 us
    slice x1 -> x0, local copies, waits for them, and re-layouts: 12.9 us -> none  [on_device(): target = target | (incoming_pos[..., column:column + 1] == labels)]
  transfers between devices with their start and end apart: 3 -> 3, of which waited for: 2 -> 2; matrix products, arithmetic and copies ran while one was open for 10% -> 6% of each run, Pallas kernels for 0% -> 0%
where the time goes in v3:
time: 762 us; the launch traced here: 760 us
  waiting for transfers between devices  547 us (72%)
  local copies, waits for them, and re-layouts  91.3 us (12%)
  Pallas kernels  40.1 us (5%)
  matrix products  33.5 us (4%)
  starting transfers between devices  28.5 us (4%)
  other arithmetic  19 us (2%)
    all_to_all x1, waiting for transfers between devices, on_device(): lax.all_to_all(row_grads.reshape(per_dst, devices, width), AXES, split_ax...  275 us
    all_to_all x1, waiting for transfers between devices, on_device(): lax.all_to_all(outgoing.reshape(per_dst, devices, width), AXES, split_axi...  273 us
    pallas_call x1, Pallas kernels, on_device(): pl.pallas_call(cluster_kernel, grid=(local_clusters,), in_specs=[pl.Block...  40.1 us
    all_to_all x1, local copies, waits for them, and re-layouts, on_device(): lax.all_to_all(row_grads.reshape(per_dst, devices, width), AXES, split_ax...  20.9 us
    all_to_all x1, local copies, waits for them, and re-layouts, on_device(): lax.all_to_all(outgoing.reshape(per_dst, devices, width), AXES, split_axi...  20.9 us
    reshape x1, local copies, waits for them, and re-layouts, on_device(): outgoing.reshape(per_dst, devices, width)  20.8 us
    reshape x1, local copies, waits for them, and re-layouts, on_device(): row_grads.reshape(per_dst, devices, width)  20.8 us
    dot_general x1, matrix products, on_device(): jnp.dot(dispatch, queries, preferred_element_type=jnp.float32)  15.4 us
  transfers between devices with their start and end apart: 3, of which 2 were waited for; matrix products, arithmetic and copies ran while one was open for 6% of the time, Pallas kernels for 0%

profile of v3, /device:TPU:10, one launch (start us, length us, event | category | flops | bytes accessed | tf_op | source)
XLA Modules:
  0.0 760.4 jit_solution(4483209582767886400)
XLA Ops:
  0.6 0.0 copy-start
  0.6 0.0 copy-start.5
  0.7 0.0 copy-start.6
  0.7 0.9 fusion.22
  1.6 5.5 compare_reduce_fusion
  7.2 0.8 fusion
  8.0 0.1 eq.71
  8.0 0.0 copy-done.5
  8.1 0.0 copy-done.6
  8.2 7.3 bitcast_compare_fusion
  15.5 0.0 copy-start.3
  15.5 3.0 fusion.29
  18.5 0.1 compare_reduce_fusion.1
  18.6 0.2 select_reduce_fusion
  18.8 0.0 copy-done.3
  18.8 0.8 select_bitcast_fusion
  19.7 2.0 copy.22
  21.6 10.9 %all-to-all-start.1 = ((s32[72,128,8]{0,2,1:T(8,128)}), s32[72,128,8]{0,2,1:T(8,128)}, u32[]{:S(2)}, u32[]{:S(2)}) async-start(s32[72,128,8]{0,2,1:T(8,128)} %copy.22), calls=%async_computation.1 | async-start | bytes 1048576 | tf_op jit(solution)/shard_map/all_to_all | solution.py:92
  32.5 0.0 copy-done
  32.5 0.0 copy-start.7
  32.6 2.2 fusion.28
  34.8 0.3 multiply_reduce_fusion
  35.1 0.0 copy-done.7
  35.1 15.4 %convolution_convert_fusion = bf16[9216,1024]{1,0:T(8,128)(2,1)} fusion(pred[9216,384]{1,0:T(32,128)(4,1)} %copy-done.3, f32[384,1024]{1,0:T(8,128)S(1)} %get-tuple-element.7, f32[1024]{0:T(1024)S(1)} %copy-done.7, f32[384]{0:T(512)S(1)} %add_rsqrt_fusion, f32[384]{0:T(512)S(1)} %broadcast_multiply_fusion.1), kind=kOutput, calls=%fused_computation.1 | convolution fusion | flops 7258767360 | bytes 23993344 | tf_op jit(solution)/shard_map/dot_general | solution.py:63
  50.5 20.8 %copy.20 = bf16[72,128,1024]{2,0,1:T(8,128)(2,1)} copy(bf16[72,128,1024]{2,1,0:T(8,128)(2,1)} %bitcast.25) | data formatting | bytes 37748736 | tf_op jit(solution)/shard_map/reshape | solution.py:90
  71.3 0.0 all-to-all-done.1
  71.3 10.2 %all-to-all-start = ((bf16[72,128,1024]{2,0,1:T(8,128)(2,1)}), bf16[72,128,1024]{2,0,1:T(8,128)(2,1)}, u32[]{:S(2)}, u32[]{:S(2)}) async-start(bf16[72,128,1024]{2,0,1:T(8,128)(2,1)} %copy.20), calls=%async_computation | async-start | bytes 37748736 | tf_op jit(solution)/shard_map/all_to_all | solution.py:89
  81.5 5.7 copy.23
  87.2 272.6 %all-to-all-done = bf16[72,128,1024]{2,0,1:T(8,128)(2,1)} async-done(((bf16[72,128,1024]{2,0,1:T(8,128)(2,1)}), bf16[72,128,1024]{2,0,1:T(8,128)(2,1)}, u32[]{:S(2)}, u32[]{:S(2)}) %all-to-all-start) | async-done | bytes 18874400 | tf_op jit(solution)/shard_map/all_to_all | solution.py:89
  359.7 0.0 copy-start.2
  359.7 20.9 %copy.21 = bf16[72,128,1024]{2,1,0:T(8,128)(2,1)} copy(bf16[72,128,1024]{2,0,1:T(8,128)(2,1)} %all-to-all-done) | data formatting | bytes 37748736 | tf_op jit(solution)/shard_map/all_to_all | solution.py:89
  380.7 0.0 copy-done.2
  380.7 40.1 %shard_map.77 = (f32[12,256,1024]{2,1,0:T(8,128)}, bf16[9216,1024]{1,0:T(8,128)(2,1)}) custom-call(bf16[9216,1024]{1,0:T(8,128)(2,1)} %bitcast.26, s32[9216,8]{1,0:T(8,128)S(1)} %bitcast.24, bf16[12,256,1024]{2,1,0:T(8,128)(2,1)} %bitcast.33), custom_call_target="tpu_custom_call" | custom-call | flops 14495514624 | bytes 56623104 | tf_op jit(solution)/shard_map/pallas_call | solution.py:98
  420.7 20.8 %copy.24 = bf16[72,128,1024]{2,0,1:T(8,128)(2,1)} copy(bf16[72,128,1024]{2,1,0:T(8,128)(2,1)} %bitcast.27) | data formatting | bytes 37748736 | tf_op jit(solution)/shard_map/reshape | solution.py:123
  441.5 7.4 all-to-all-start.2
  449.0 3.6 broadcast_compare_fusion
  452.6 274.6 %all-to-all-done.2 = bf16[72,128,1024]{2,0,1:T(8,128)(2,1)} async-done(((bf16[72,128,1024]{2,0,1:T(8,128)(2,1)}), bf16[72,128,1024]{2,0,1:T(8,128)(2,1)}, u32[]{:S(2)}, u32[]{:S(2)}) %all-to-all-start.2) | async-done | bytes 18874400 | tf_op jit(solution)/shard_map/all_to_all | solution.py:122
  727.2 0.0 copy-start.4
  727.2 20.9 %copy.25 = bf16[72,128,1024]{2,1,0:T(8,128)(2,1)} copy(bf16[72,128,1024]{2,0,1:T(8,128)(2,1)} %all-to-all-done.2) | data formatting | bytes 37748736 | tf_op jit(solution)/shard_map/all_to_all | solution.py:122
  748.2 0.0 copy-done.4
  748.2 0.0 copy-start.1
  748.2 12.2 %fusion.30 = f32[384,1024]{1,0:T(8,128)} fusion(pred[9216,384]{1,0:T(32,128)(4,1)S(1)} %bitcast.31, bf16[9216,1024]{1,0:T(8,128)(2,1)} %bitcast.28), kind=kOutput, calls=%fused_computation.71 | convolution fusion | flops 7247757312 | bytes 23986176 | tf_op jit(solution)/shard_map/dot_general | solution.py:125
  760.4 0.0 copy-done.1
  (12 shorter events, 0.1 us)
Async XLA Ops:
  0.6 31.9 %copy-start = (bf16[1024,1024]{1,0:T(8,128)(2,1)S(1)}, bf16[1024,1024]{1,0:T(8,128)(2,1)}, u32[]{:S(2)}) copy-start(bf16[1024,1024]{1,0:T(8,128)(2,1)} %param.7) | copy-start | bytes 6291460
  0.6 7.4 copy-start.5
  0.7 7.4 copy-start.6
  15.5 3.3 copy-start.3
  21.6 49.6 %all-to-all-start.1 = ((s32[72,128,8]{0,2,1:T(8,128)}), s32[72,128,8]{0,2,1:T(8,128)}, u32[]{:S(2)}, u32[]{:S(2)}) async-start(s32[72,128,8]{0,2,1:T(8,128)} %copy.22), calls=%async_computation.1 | async-start | bytes 1048576 | tf_op jit(solution)/shard_map/all_to_all | solution.py:92
  32.5 2.5 copy-start.7
  71.3 288.5 %all-to-all-start = ((bf16[72,128,1024]{2,0,1:T(8,128)(2,1)}), bf16[72,128,1024]{2,0,1:T(8,128)(2,1)}, u32[]{:S(2)}, u32[]{:S(2)}) async-start(bf16[72,128,1024]{2,0,1:T(8,128)(2,1)} %copy.20), calls=%async_computation | async-start | bytes 37748736 | tf_op jit(solution)/shard_map/all_to_all | solution.py:89
  359.7 20.9 %copy-start.2 = (s32[72,128,8]{2,1,0:T(8,128)S(1)}, s32[72,128,8]{2,1,0:T(8,128)}, u32[]{:S(2)}) copy-start(s32[72,128,8]{2,1,0:T(8,128)} %copy.23) | copy-start | bytes 884740
  441.5 285.7 %all-to-all-start.2 = ((bf16[72,128,1024]{2,0,1:T(8,128)(2,1)}), bf16[72,128,1024]{2,0,1:T(8,128)(2,1)}, u32[]{:S(2)}, u32[]{:S(2)}) async-start(bf16[72,128,1024]{2,0,1:T(8,128)(2,1)} %copy.24), calls=%async_computation.2 | async-start | bytes 37748736 | tf_op jit(solution)/shard_map/all_to_all | solution.py:122
  727.2 20.9 %copy-start.4 = (pred[12,6,128,384]{3,2,1,0:T(32,128)(4,1)S(1)}, pred[12,6,128,384]{3,2,1,0:T(32,128)(4,1)}, u32[]{:S(2)}) copy-start(pred[12,6,128,384]{3,2,1,0:T(32,128)(4,1)} %broadcast_compare_fusion) | copy-start | bytes 10616836
  748.2 12.2 %copy-start.1 = (bf16[1024,1024]{1,0:T(8,128)(2,1)S(1)}, bf16[1024,1024]{1,0:T(8,128)(2,1)}, u32[]{:S(2)}) copy-start(bf16[1024,1024]{1,0:T(8,128)(2,1)} %param.7) | copy-start | bytes 6291460

commit v4 on v3

--- a/solution.py
+++ b/solution.py
@@ -58,7 +58,9 @@
     level = jnp.where(member, rank, float(CAP + 1)).astype(jnp.bfloat16)
     level = level.reshape(local_clusters, 1, devices, query_count)
     slot_rank = jnp.arange(CAP, dtype=jnp.int32).astype(jnp.bfloat16)[None, :, None, None]
-    dispatch = (level == slot_rank).astype(jnp.bfloat16).reshape(slots, query_count)
+    dispatch = (
+        (level == slot_rank).astype(jnp.bfloat16).transpose(2, 0, 1, 3).reshape(slots, query_count)
+    )
 
     outgoing = jnp.dot(dispatch, queries, preferred_element_type=jnp.float32).astype(jnp.bfloat16)
     parts = jnp.concatenate(
@@ -77,7 +79,7 @@
     ).astype(jnp.int32)
     occupied = gathered[:, p_base + 2 * positive_count :] > 0.5
     row = jnp.arange(slots, dtype=jnp.int32)[:, None]
-    slot_cluster = (row % devices) * local_clusters + row // (CAP * devices)
+    slot_cluster = row // CAP
     slot_k = jnp.sum(
         jnp.where(slot_list == slot_cluster, jnp.arange(shortlist_size, dtype=jnp.int32), 0),
         axis=1, keepdims=True,
@@ -87,12 +89,12 @@
     local_positive = jnp.where(inside, offsets, -1).astype(jnp.int32)
 
     incoming = lax.all_to_all(
-        outgoing.reshape(per_dst, devices, width), AXES, split_axis=1, concat_axis=1, tiled=True
-    ).reshape(slots, width)
+        outgoing.reshape(devices, per_dst, width), AXES, split_axis=0, concat_axis=0, tiled=True
+    ).transpose(1, 0, 2).reshape(slots, width)
     incoming_pos = lax.all_to_all(
-        local_positive.reshape(per_dst, devices, positive_count),
-        AXES, split_axis=1, concat_axis=1, tiled=True,
-    ).reshape(slots, positive_count)
+        local_positive.reshape(devices, per_dst, positive_count),
+        AXES, split_axis=0, concat_axis=0, tiled=True,
+    ).transpose(1, 0, 2).reshape(slots, positive_count)
     by_cluster = jnp.transpose(label_weight, (1, 0, 2))
     rows_per_cluster = CAP * devices
     grad, row_grads = pl.pallas_call(
@@ -119,8 +121,9 @@
         ),
     )(incoming, incoming_pos, by_cluster)
     weight_grad = jnp.transpose(grad, (1, 0, 2))
+    row_grads = row_grads.reshape(per_dst, devices, width).transpose(1, 0, 2)
     returned = lax.all_to_all(
-        row_grads.reshape(per_dst, devices, width), AXES, split_axis=1, concat_axis=1, tiled=True
+        row_grads, AXES, split_axis=0, concat_axis=0, tiled=True
     ).reshape(slots, width)
     query_grad = lax.dot_general(
         dispatch, returned, (((0,), (0,)), ((), ())), preferred_element_type=jnp.float32

time: 762 us -> 747 us (0.980); the launches traced: 760 us -> 737 us
  waiting for transfers between devices: 547 us -> 531 us
  local copies, waits for them, and re-layouts: 91.3 us -> 81.5 us
  matrix products: 33.5 us -> 42 us
    all_to_all x3 -> x0, local copies, waits for them, and re-layouts: 47.6 us -> none  [the longest x1 20.9 us: on_device(): lax.all_to_all(row_grads.reshape(per_dst, devices, width), AXES, split_ax...]
    eq x2 -> x6, local copies, waits for them, and re-layouts: 0.09 us -> 32.1 us  [on_device(): level == slot_rank]
    transpose x0 -> x2, local copies, waits for them, and re-layouts: none -> 25.7 us  [the longest x1 20.9 us: on_device(): incoming = lax.all_to_all(outgoing.reshape(devices, per_dst, width), AXES...]
    reshape x3, local copies, waits for them, and re-layouts: 43.5 us -> 22.5 us  [the longest x1 20.9 us: on_device(): row_grads = row_grads.reshape(per_dst, devices, width).transpose(1, 0, 2)]
    all_to_all x3, waiting for transfers between devices: 547 us -> 531 us  [the longest x1 271 us: on_device(): lax.all_to_all(outgoing.reshape(devices, per_dst, width), AXES, split_axi...]
where the time goes in v4:
time: 747 us; the launch traced here: 737 us
  waiting for transfers between devices  531 us (71%)
  local copies, waits for them, and re-layouts  81.5 us (11%)
  matrix products  42 us (6%)
  Pallas kernels  40.1 us (5%)
  starting transfers between devices  28.8 us (4%)
  other arithmetic  12.9 us (2%)
    all_to_all x1, waiting for transfers between devices, on_device(): lax.all_to_all(outgoing.reshape(devices, per_dst, width), AXES, split_axi...  271 us
    all_to_all x1, waiting for transfers between devices, on_device(): lax.all_to_all(row_grads, AXES, split_axis=0, concat_axis=0, tiled=True)  260 us
    pallas_call x1, Pallas kernels, on_device(): pl.pallas_call(cluster_kernel, grid=(local_clusters,), in_specs=[pl.Block...  40.1 us
    eq x6, local copies, waits for them, and re-layouts, on_device(): level == slot_rank  32.1 us
    transpose x1, local copies, waits for them, and re-layouts, on_device(): incoming = lax.all_to_all(outgoing.reshape(devices, per_dst, width), AXES...  20.9 us
    reshape x1, local copies, waits for them, and re-layouts, on_device(): row_grads = row_grads.reshape(per_dst, devices, width).transpose(1, 0, 2)  20.9 us
    dot_general x1, matrix products, on_device(): jnp.dot(dispatch, queries, preferred_element_type=jnp.float32)  19.4 us
  transfers between devices with their start and end apart: 3, of which 2 were waited for; matrix products, arithmetic and copies ran while one was open for 6% of the time, Pallas kernels for 0%

profile of v4, /device:TPU:10, one launch (start us, length us, event | category | flops | bytes accessed | tf_op | source)
XLA Modules:
  0.0 737.3 jit_solution(16980755834385579768)
XLA Ops:
  0.6 0.0 copy-start
  0.7 0.9 fusion.20
  1.6 5.5 compare_reduce_fusion
  7.2 0.8 fusion.5
  7.9 1.9 copy.20
  9.8 6.7 eq.68
  16.5 0.0 copy-start.5
  16.5 0.0 copy-start.6
  16.5 12.7 %eq.72 = bf16[9216,384]{1,0:T(8,128)(2,1)} reshape(bf16[128,12,6,384]{3,2,1,0:T(8,128)(2,1)} %eq.68) | data formatting | bytes 14155776 | tf_op jit(solution)/shard_map/eq | solution.py:62
  29.2 0.1 eq.73
  29.3 0.5 eq.74
  29.8 0.0 copy-done.5
  29.8 0.0 copy-done.6
  29.9 6.2 fusion
  36.1 0.1 compare_reduce_fusion.1
  36.2 0.2 select_reduce_fusion
  36.4 0.1 and_select_fusion
  36.6 0.5 reshape.123
  37.1 1.1 copy.22
  38.2 10.4 %all-to-all-start.1 = ((s32[128,72,8]{1,2,0:T(8,128)}), s32[128,72,8]{1,2,0:T(8,128)S(1)}, u32[]{:S(2)}, u32[]{:S(2)}) async-start(s32[128,72,8]{1,2,0:T(8,128)} %copy.22), calls=%async_computation.1 | async-start | bytes 1048576 | tf_op jit(solution)/shard_map/all_to_all | solution.py:94
  48.6 0.0 copy-done
  48.6 0.0 copy-start.7
  48.6 2.2 fusion.26
  50.8 0.0 copy-start.4
  50.9 1.1 copy-done.4
  52.0 0.3 multiply_reduce_fusion
  52.3 0.0 copy-done.7
  52.3 19.4 %convolution_convert_fusion = bf16[9216,1024]{1,0:T(8,128)(2,1)} fusion(bf16[9216,384]{1,0:T(8,128)(2,1)} %eq.72, bf16[9216]{0:T(1024)(128)(2,1)S(1)} %eq.74, f32[384,1024]{1,0:T(8,128)} %copy-done.4, f32[1024]{0:T(1024)S(1)} %copy-done.7, f32[384]{0:T(512)S(1)} %add_rsqrt_fusion, f32[384]{0:T(512)S(1)} %broadcast_multiply_fusion.1), kind=kOutput, calls=%fused_computation.2 | convolution fusion | flops 7262306304 | bytes 27550720 | tf_op jit(solution)/shard_map/dot_general | solution.py:65
  71.7 0.0 all-to-all-done.1
  71.7 10.6 %all-to-all-start = ((bf16[128,72,1024]{2,1,0:T(8,128)(2,1)}), bf16[128,72,1024]{2,1,0:T(8,128)(2,1)}, u32[]{:S(2)}, u32[]{:S(2)}) async-start(bf16[128,72,1024]{2,1,0:T(8,128)(2,1)} %bitcast.28), calls=%async_computation | async-start | bytes 37748736 | tf_op jit(solution)/shard_map/all_to_all | solution.py:91
  82.2 4.8 copy.23
  87.0 270.9 %all-to-all-done = bf16[128,72,1024]{2,1,0:T(8,128)(2,1)} async-done(((bf16[128,72,1024]{2,1,0:T(8,128)(2,1)}), bf16[128,72,1024]{2,1,0:T(8,128)(2,1)}, u32[]{:S(2)}, u32[]{:S(2)}) %all-to-all-start) | async-done | bytes 18874400 | tf_op jit(solution)/shard_map/all_to_all | solution.py:91
  358.0 0.0 copy-start.2
  358.0 20.9 %copy.21 = bf16[72,128,1024]{2,1,0:T(8,128)(2,1)} copy(bf16[72,128,1024]{2,0,1:T(8,128)(2,1)} %bitcast.5) | data formatting | bytes 37748736 | tf_op jit(solution)/shard_map/transpose | solution.py:93
  378.9 0.0 copy-done.2
  378.9 40.1 %shard_map.77 = (f32[12,256,1024]{2,1,0:T(8,128)}, bf16[9216,1024]{1,0:T(8,128)(2,1)}) custom-call(bf16[9216,1024]{1,0:T(8,128)(2,1)} %bitcast.29, s32[9216,8]{1,0:T(8,128)S(1)} %bitcast.26, bf16[12,256,1024]{2,1,0:T(8,128)(2,1)} %bitcast.34), custom_call_target="tpu_custom_call" | custom-call | flops 14495514624 | bytes 56623104 | tf_op jit(solution)/shard_map/pallas_call | solution.py:100
  419.0 20.9 %copy.26 = bf16[72,128,1024]{2,0,1:T(8,128)(2,1)} copy(bf16[72,128,1024]{2,1,0:T(8,128)(2,1)} %bitcast.30) | data formatting | bytes 37748736 | tf_op jit(solution)/shard_map/reshape | solution.py:124
  439.8 0.0 copy-start.3
  439.8 7.8 %all-to-all-start.2 = ((bf16[128,72,1024]{2,1,0:T(8,128)(2,1)}), bf16[128,72,1024]{2,1,0:T(8,128)(2,1)}, u32[]{:S(2)}, u32[]{:S(2)}) async-start(bf16[128,72,1024]{2,1,0:T(8,128)(2,1)} %bitcast.27), calls=%async_computation.2 | async-start | bytes 37748736 | tf_op jit(solution)/shard_map/all_to_all | solution.py:125
  447.7 0.0 copy-done.3
  447.7 5.5 broadcast_compare_fusion
  453.2 10.3 %eq.71 = pred[9216,384]{1,0:T(32,128)(4,1)} reshape(pred[128,12,6,384]{3,2,1,0:T(8,128)(4,1)} %broadcast_compare_fusion) | data formatting | bytes 7077888 | tf_op jit(solution)/shard_map/eq | solution.py:62
  463.5 259.9 %all-to-all-done.2 = bf16[128,72,1024]{2,1,0:T(8,128)(2,1)} async-done(((bf16[128,72,1024]{2,1,0:T(8,128)(2,1)}), bf16[128,72,1024]{2,1,0:T(8,128)(2,1)}, u32[]{:S(2)}, u32[]{:S(2)}) %all-to-all-start.2) | async-done | bytes 18874400 | tf_op jit(solution)/shard_map/all_to_all | solution.py:125
  723.4 0.0 copy-start.1
  723.4 13.4 %fusion.27 = f32[384,1024]{1,0:T(8,128)} fusion(pred[9216,384]{1,0:T(32,128)(4,1)} %eq.71, bf16[9216,1024]{1,0:T(8,128)(2,1)} %bitcast.12), kind=kOutput, calls=%fused_computation.67 | convolution fusion | flops 7247757312 | bytes 23986176 | tf_op jit(solution)/shard_map/dot_general | solution.py:128
  736.9 0.0 copy-done.1
  (11 shorter events, 0.1 us)
Async XLA Ops:
  0.6 48.0 %copy-start = (bf16[1024,1024]{1,0:T(8,128)(2,1)S(1)}, bf16[1024,1024]{1,0:T(8,128)(2,1)}, u32[]{:S(2)}) copy-start(bf16[1024,1024]{1,0:T(8,128)(2,1)} %param.7) | copy-start | bytes 6291460
  16.5 13.2 %copy-start.5 = (s32[384,16]{0,1:T(8,128)S(1)}, s32[384,16]{0,1:T(8,128)}, u32[]{:S(2)}) copy-start(s32[384,16]{0,1:T(8,128)} %param.9) | copy-start | bytes 73732
  16.5 13.3 %copy-start.6 = (s32[384,8]{0,1:T(8,128)S(1)}, s32[384,8]{0,1:T(8,128)}, u32[]{:S(2)}) copy-start(s32[384,8]{0,1:T(8,128)} %param.10) | copy-start | bytes 36868
  38.2 33.5 %all-to-all-start.1 = ((s32[128,72,8]{1,2,0:T(8,128)}), s32[128,72,8]{1,2,0:T(8,128)S(1)}, u32[]{:S(2)}, u32[]{:S(2)}) async-start(s32[128,72,8]{1,2,0:T(8,128)} %copy.22), calls=%async_computation.1 | async-start | bytes 1048576 | tf_op jit(solution)/shard_map/all_to_all | solution.py:94
  48.6 3.7 copy-start.7
  50.8 1.1 copy-start.4
  71.7 286.3 %all-to-all-start = ((bf16[128,72,1024]{2,1,0:T(8,128)(2,1)}), bf16[128,72,1024]{2,1,0:T(8,128)(2,1)}, u32[]{:S(2)}, u32[]{:S(2)}) async-start(bf16[128,72,1024]{2,1,0:T(8,128)(2,1)} %bitcast.28), calls=%async_computation | async-start | bytes 37748736 | tf_op jit(solution)/shard_map/all_to_all | solution.py:91
  358.0 20.9 %copy-start.2 = (s32[72,128,8]{2,1,0:T(8,128)S(1)}, s32[72,128,8]{2,1,0:T(8,128)}, u32[]{:S(2)}) copy-start(s32[72,128,8]{2,1,0:T(8,128)} %copy.23) | copy-start | bytes 884740
  439.8 7.9 %copy-start.3 = (bf16[128,12,384]{2,1,0:T(8,128)(2,1)S(1)}, bf16[128,12,384]{2,1,0:T(8,128)(2,1)}, u32[]{:S(2)}) copy-start(bf16[128,12,384]{2,1,0:T(8,128)(2,1)} %copy.20) | copy-start | bytes 3538948
  439.8 283.6 %all-to-all-start.2 = ((bf16[128,72,1024]{2,1,0:T(8,128)(2,1)}), bf16[128,72,1024]{2,1,0:T(8,128)(2,1)}, u32[]{:S(2)}, u32[]{:S(2)}) async-start(bf16[128,72,1024]{2,1,0:T(8,128)(2,1)} %bitcast.27), calls=%async_computation.2 | async-start | bytes 37748736 | tf_op jit(solution)/shard_map/all_to_all | solution.py:125
  723.4 13.4 %copy-start.1 = (bf16[1024,1024]{1,0:T(8,128)(2,1)S(1)}, bf16[1024,1024]{1,0:T(8,128)(2,1)}, u32[]{:S(2)}) copy-start(bf16[1024,1024]{1,0:T(8,128)(2,1)} %param.7) | copy-start | bytes 6291460

commit v5 on v4

--- a/solution.py
+++ b/solution.py
@@ -6,6 +6,7 @@
 from jax.experimental.pallas import tpu as pltpu
 
 CAP = 6
+CHUNKS = (8, 4)
 AXES = ("row", "col")
 
 
@@ -17,7 +18,8 @@
     return (centred * lax.rsqrt(spread + 1e-05) * norm_gain).astype(jnp.bfloat16)
 
 
-def cluster_kernel(incoming_ref, positive_ref, weight_ref, grad_ref, rows_ref):
+def cluster_kernel(incoming_ref, positive_ref, weight_ref, *refs):
+    grad_ref, rows_ref = refs[-2:]
     block = weight_ref[0]
     x = incoming_ref[...]
     scores = lax.dot_general(
@@ -62,7 +64,6 @@
         (level == slot_rank).astype(jnp.bfloat16).transpose(2, 0, 1, 3).reshape(slots, query_count)
     )
 
-    outgoing = jnp.dot(dispatch, queries, preferred_element_type=jnp.float32).astype(jnp.bfloat16)
     parts = jnp.concatenate(
         [shortlist // 256, shortlist % 256, positives // 256, positives % 256,
          jnp.ones((query_count, 1), jnp.int32)],
@@ -88,46 +89,61 @@
     inside = (offsets >= 0) & (offsets < block_labels) & occupied
     local_positive = jnp.where(inside, offsets, -1).astype(jnp.int32)
 
-    incoming = lax.all_to_all(
-        outgoing.reshape(devices, per_dst, width), AXES, split_axis=0, concat_axis=0, tiled=True
-    ).transpose(1, 0, 2).reshape(slots, width)
     incoming_pos = lax.all_to_all(
         local_positive.reshape(devices, per_dst, positive_count),
         AXES, split_axis=0, concat_axis=0, tiled=True,
     ).transpose(1, 0, 2).reshape(slots, positive_count)
     by_cluster = jnp.transpose(label_weight, (1, 0, 2))
     rows_per_cluster = CAP * devices
-    grad, row_grads = pl.pallas_call(
-        cluster_kernel,
-        grid=(local_clusters,),
-        in_specs=[
-            pl.BlockSpec((rows_per_cluster, width), lambda c: (c, 0)),
-            pl.BlockSpec((rows_per_cluster, positive_count), lambda c: (c, 0)),
-            pl.BlockSpec((1, block_labels, width), lambda c: (c, 0, 0)),
-        ],
-        out_specs=[
-            pl.BlockSpec((1, block_labels, width), lambda c: (c, 0, 0)),
-            pl.BlockSpec((rows_per_cluster, width), lambda c: (c, 0)),
-        ],
-        out_shape=[
-            jax.ShapeDtypeStruct((local_clusters, block_labels, width), jnp.float32),
-            jax.ShapeDtypeStruct((slots, width), jnp.bfloat16),
-        ],
-        compiler_params=pltpu.CompilerParams(vmem_limit_bytes=48 * 1024 * 1024),
-        cost_estimate=pl.CostEstimate(
-            flops=6 * slots * block_labels * width,
-            transcendentals=slots * block_labels,
-            bytes_accessed=2 * slots * width * 2 + local_clusters * block_labels * width * 6,
-        ),
-    )(incoming, incoming_pos, by_cluster)
+    dispatch = dispatch.reshape(devices, per_dst, query_count)
+    query_grad = jnp.zeros((query_count, width), jnp.float32)
+    grad = None
+    first = 0
+    for count in CHUNKS:
+        rows = count * CAP
+        part = dispatch[:, first * CAP : first * CAP + rows, :].reshape(devices * rows, query_count)
+        outgoing = jnp.dot(part, queries, preferred_element_type=jnp.float32).astype(jnp.bfloat16)
+        incoming = lax.all_to_all(
+            outgoing.reshape(devices, rows, width), AXES, split_axis=0, concat_axis=0, tiled=True
+        ).transpose(1, 0, 2).reshape(devices * rows, width)
+        operands = [incoming, incoming_pos, by_cluster]
+        aliases = {}
+        if grad is not None:
+            operands.append(grad)
+            aliases = {3: 0}
+        grad, row_grads = pl.pallas_call(
+            cluster_kernel,
+            grid=(count,),
+            in_specs=[
+                pl.BlockSpec((rows_per_cluster, width), lambda c: (c, 0)),
+                pl.BlockSpec((rows_per_cluster, positive_count), lambda c, f=first: (c + f, 0)),
+                pl.BlockSpec((1, block_labels, width), lambda c, f=first: (c + f, 0, 0)),
+            ] + ([pl.BlockSpec(memory_space=pl.ANY)] if aliases else []),
+            out_specs=[
+                pl.BlockSpec((1, block_labels, width), lambda c, f=first: (c + f, 0, 0)),
+                pl.BlockSpec((rows_per_cluster, width), lambda c: (c, 0)),
+            ],
+            out_shape=[
+                jax.ShapeDtypeStruct((local_clusters, block_labels, width), jnp.float32),
+                jax.ShapeDtypeStruct((devices * rows, width), jnp.bfloat16),
+            ],
+            input_output_aliases=aliases,
+            compiler_params=pltpu.CompilerParams(vmem_limit_bytes=48 * 1024 * 1024),
+            cost_estimate=pl.CostEstimate(
+                flops=6 * devices * rows * block_labels * width,
+                transcendentals=devices * rows * block_labels,
+                bytes_accessed=4 * devices * rows * width + count * block_labels * width * 6,
+            ),
+        )(*operands)
+        row_grads = row_grads.reshape(rows, devices, width).transpose(1, 0, 2)
+        returned = lax.all_to_all(
+            row_grads, AXES, split_axis=0, concat_axis=0, tiled=True
+        ).reshape(devices * rows, width)
+        query_grad = query_grad + lax.dot_general(
+            part, returned, (((0,), (0,)), ((), ())), preferred_element_type=jnp.float32
+        )
+        first += count
     weight_grad = jnp.transpose(grad, (1, 0, 2))
-    row_grads = row_grads.reshape(per_dst, devices, width).transpose(1, 0, 2)
-    returned = lax.all_to_all(
-        row_grads, AXES, split_axis=0, concat_axis=0, tiled=True
-    ).reshape(slots, width)
-    query_grad = lax.dot_general(
-        dispatch, returned, (((0,), (0,)), ((), ())), preferred_element_type=jnp.float32
-    )
     return (query_grad, weight_grad)
 
 

time: 747 us -> 616 us (0.82)
  the two profiles are of different devices: /device:TPU:10 before, /device:TPU:2 now
where the time goes in v5:
time: 616 us; the launch traced here: 607 us
  waiting for transfers between devices  341 us (55%)
  local copies, waits for them, and re-layouts  96.3 us (16%)
  matrix products  58.5 us (9%)
  starting transfers between devices  57.5 us (9%)
  Pallas kernels  42.7 us (7%)
  other arithmetic  9.22 us (1%)
    all_to_all x2, waiting for transfers between devices, on_device(): lax.all_to_all(row_grads, AXES, split_axis=0, concat_axis=0, tiled=True)  178 us
    all_to_all x2, waiting for transfers between devices, on_device(): lax.all_to_all(outgoing.reshape(devices, rows, width), AXES, split_axis=0...  163 us
    pallas_call x2, Pallas kernels, on_device(): pl.pallas_call(cluster_kernel, grid=(count,), in_specs=[pl.BlockSpec((row...  42.7 us
    dot_general x2, matrix products, on_device(): lax.dot_general(part, returned, (((0,), (0,)), ((), ())), preferred_eleme...  33.6 us
    all_to_all x2, starting transfers between devices, on_device(): lax.all_to_all(outgoing.reshape(devices, rows, width), AXES, split_axis=0...  25.5 us
    transpose x2, local copies, waits for them, and re-layouts, on_device(): incoming = lax.all_to_all(outgoing.reshape(devices, rows, width), AXES, s...  23.6 us
    reshape x2, local copies, waits for them, and re-layouts, on_device(): row_grads = row_grads.reshape(rows, devices, width).transpose(1, 0, 2)  23.6 us
    eq x7, local copies, waits for them, and re-layouts, on_device(): level == slot_rank  21.9 us
  transfers between devices with their start and end apart: 5, of which 4 were waited for; matrix products, arithmetic and copies ran while one was open for 18% of the time, Pallas kernels for 7%

profile of v5, /device:TPU:2, one launch (start us, length us, event | category | flops | bytes accessed | tf_op | source)
XLA Modules:
  0.0 606.7 jit_solution(17633125881400712640)
XLA Ops:
  0.6 0.0 copy-start
  0.6 0.0 copy-start.8
  0.7 0.0 copy-start.9
  0.7 0.9 fusion.21
  1.6 5.5 compare_reduce_fusion
  7.2 0.8 fusion.7
  8.0 0.0 copy-done.8
  8.0 0.0 copy-start.5
  8.0 0.0 copy-done.9
  8.1 0.9 copy-done.5
  9.0 1.9 copy.32
  10.9 6.7 %eq.66 = bf16[128,12,6,384]{3,2,1,0:T(8,128)(2,1)} broadcast(bf16[128,12,384]{2,1,0:T(8,128)(2,1)} %copy.32), dimensions={0,1,3} | broadcast | bytes 8257536 | tf_op jit(solution)/shard_map/eq | solution.py:64
  17.6 12.6 %eq.72 = bf16[9216,384]{1,0:T(8,128)(2,1)} reshape(bf16[128,12,6,384]{3,2,1,0:T(8,128)(2,1)} %eq.66) | data formatting | bytes 14155776 | tf_op jit(solution)/shard_map/eq | solution.py:64
  30.2 0.1 eq.73
  30.3 0.5 eq.74
  30.8 6.2 %fusion = f32[9216,49]{0,1:T(8,128)S(1)} fusion(bf16[384,49]{0,1:T(8,128)(2,1)S(1)} %constant_dynamic-update-slice_fusion, bf16[9216,384]{1,0:T(8,128)(2,1)} %eq.72, bf16[9216]{0:T(1024)(128)(2,1)S(1)} %eq.74), kind=kOutput, calls=%fused_computation.1 | convolution fusion | flops 350355456 | bytes 8940288 | tf_op jit(solution)/shard_map/dot_general | solution.py:72
  37.0 0.1 compare_reduce_fusion.1
  37.1 0.2 select_reduce_fusion
  37.4 0.1 and_select_fusion
  37.5 0.5 reshape.110
  38.0 1.1 copy.36
  39.1 11.0 %all-to-all-start.1 = ((s32[128,72,8]{1,2,0:T(8,128)}), s32[128,72,8]{1,2,0:T(8,128)}, u32[]{:S(2)}, u32[]{:S(2)}) async-start(s32[128,72,8]{1,2,0:T(8,128)} %copy.36), calls=%async_computation.1 | async-start | bytes 1048576 | tf_op jit(solution)/shard_map/all_to_all | solution.py:92
  50.1 1.7 copy.44
  51.8 0.1 eq.69
  51.9 1.9 bitcast_compare_fusion
  53.8 0.0 copy-start.4
  53.8 1.7 copy-done.4
  55.6 2.4 slice.28
  57.9 0.0 copy-start.10
  58.0 6.6 %copy.34 = pred[128,48,384]{2,1,0:T(8,128)(4,1)} copy(pred[128,48,384]{0,2,1:T(8,128)(4,1)} %slice.28) | data formatting | bytes 4718592 | tf_op jit(solution)/shard_map/slice | solution.py:104
  64.6 0.0 copy-done
  64.6 0.0 copy-done.10
  64.6 0.0 copy-start.6
  64.6 0.0 copy-start.11
  64.6 1.1 fusion.27
  65.7 0.3 multiply_reduce_fusion
  66.0 0.8 copy-done.7
  66.8 0.0 copy-done.6
  66.8 0.0 copy-done.11
  66.8 9.9 %convolution_convert_fusion = bf16[6144,1024]{1,0:T(8,128)(2,1)} fusion(pred[6144,384]{1,0:T(8,128)(4,1)S(1)} %bitcast.57, f32[384,1024]{1,0:T(8,128)S(1)} %get-tuple-element.11, f32[1024]{0:T(1024)S(1)} %copy-done.11, f32[384]{0:T(512)S(1)} %add_rsqrt_fusion, f32[384]{0:T(512)S(1)} %broadcast_multiply_fusion.1), kind=kOutput, calls=%fused_computation.6 | convolution fusion | flops 4839702528 | bytes 16522240 | tf_op jit(solution)/shard_map/dot_general | solution.py:105
  76.7 0.0 all-to-all-done.1
  76.7 10.5 %all-to-all-start = ((bf16[128,48,1024]{2,1,0:T(8,128)(2,1)}), bf16[128,48,1024]{2,1,0:T(8,128)(2,1)}, u32[]{:S(2)}, u32[]{:S(2)}) async-start(bf16[128,48,1024]{2,1,0:T(8,128)(2,1)} %bitcast.48), calls=%async_computation | async-start | bytes 25165824 | tf_op jit(solution)/shard_map/all_to_all | solution.py:106
  87.2 1.3 slice.34
  88.6 2.0 copy.40
  90.6 6.9 %convolution_convert_fusion.1 = bf16[3072,1024]{1,0:T(8,128)(2,1)} fusion(pred[3072,384]{1,0:T(8,128)(4,1)S(1)} %bitcast.58, f32[384,1024]{1,0:T(8,128)} %copy-done.7, f32[1024]{0:T(1024)S(1)} %copy-done.11, f32[384]{0:T(512)S(1)} %add_rsqrt_fusion, f32[384]{0:T(512)S(1)} %broadcast_multiply_fusion.1), kind=kOutput, calls=%fused_computation.11 | convolution fusion | flops 2420637696 | bytes 9051136 | tf_op jit(solution)/shard_map/dot_general | solution.py:105
  97.5 150.1 %all-to-all-done = bf16[128,48,1024]{2,1,0:T(8,128)(2,1)} async-done(((bf16[128,48,1024]{2,1,0:T(8,128)(2,1)}), bf16[128,48,1024]{2,1,0:T(8,128)(2,1)}, u32[]{:S(2)}, u32[]{:S(2)}) %all-to-all-start) | async-done | bytes 12582944 | tf_op jit(solution)/shard_map/all_to_all | solution.py:106
  247.6 14.9 %all-to-all-start.3 = ((bf16[128,24,1024]{2,1,0:T(8,128)(2,1)}), bf16[128,24,1024]{2,1,0:T(8,128)(2,1)}, u32[]{:S(2)}, u32[]{:S(2)}) async-start(bf16[128,24,1024]{2,1,0:T(8,128)(2,1)} %bitcast.53), calls=%async_computation.3 | async-start | bytes 12582912 | tf_op jit(solution)/shard_map/all_to_all | solution.py:106
  262.5 5.8 copy.37
  268.3 14.7 %copy.35 = bf16[48,128,1024]{2,1,0:T(8,128)(2,1)} copy(bf16[48,128,1024]{2,0,1:T(8,128)(2,1)} %bitcast.7) | data formatting | bytes 25165824 | tf_op jit(solution)/shard_map/transpose | solution.py:108
  283.1 0.0 copy-done.2
  283.1 27.6 %shard_map.77 = (f32[12,256,1024]{2,1,0:T(8,128)}, bf16[6144,1024]{1,0:T(8,128)(2,1)}) custom-call(bf16[6144,1024]{1,0:T(8,128)(2,1)} %bitcast.49, s32[9216,8]{1,0:T(8,128)S(1)} %bitcast.42, bf16[12,256,1024]{2,1,0:T(8,128)(2,1)} %bitcast.51), custom_call_target="tpu_custom_call" | custom-call | flops 9663676416 | bytes 37748736 | tf_op jit(solution)/shard_map/pallas_call | solution.py:114
  310.6 14.6 %copy.54 = bf16[48,128,1024]{2,0,1:T(8,128)(2,1)} copy(bf16[48,128,1024]{2,1,0:T(8,128)(2,1)} %bitcast.50) | data formatting | bytes 25165824 | tf_op jit(solution)/shard_map/reshape | solution.py:138
  325.3 13.4 %all-to-all-done.3 = bf16[128,24,1024]{2,1,0:T(8,128)(2,1)} async-done(((bf16[128,24,1024]{2,1,0:T(8,128)(2,1)}), bf16[128,24,1024]{2,1,0:T(8,128)(2,1)}, u32[]{:S(2)}, u32[]{:S(2)}) %all-to-all-start.3) | async-done | bytes 6291488 | tf_op jit(solution)/shard_map/all_to_all | solution.py:106
  338.6 5.7 all-to-all-start.2
  344.3 8.9 %copy.41 = bf16[24,128,1024]{2,1,0:T(8,128)(2,1)} copy(bf16[24,128,1024]{2,0,1:T(8,128)(2,1)} %bitcast.17) | data formatting | bytes 12582912 | tf_op jit(solution)/shard_map/transpose | solution.py:108
  353.2 2.3 copy-done.3
  355.5 15.2 %shard_map.78 = (f32[12,256,1024]{2,1,0:T(8,128)}, bf16[3072,1024]{1,0:T(8,128)(2,1)}) custom-call(bf16[3072,1024]{1,0:T(8,128)(2,1)} %bitcast.46, s32[9216,8]{1,0:T(8,128)S(1)} %bitcast.43, bf16[12,256,1024]{2,1,0:T(8,128)(2,1)} %bitcast.52, f32[12,256,1024]{2,1,0:T(8,128)} %get-tuple-element.7.refs_0_), custom_call_target="tpu_custom_call", output_to_operand_aliasing={{0}: (3, {})} | custom-call | flops 4831838208 | bytes 18874368 | tf_op jit(solution)/shard_map/pallas_call | solution.py:114
  370.7 9.0 %copy.55 = bf16[24,128,1024]{2,0,1:T(8,128)(2,1)} copy(bf16[24,128,1024]{2,1,0:T(8,128)(2,1)} %bitcast.54) | data formatting | bytes 12582912 | tf_op jit(solution)/shard_map/reshape | solution.py:138
  379.6 125.0 %all-to-all-done.2 = bf16[128,48,1024]{2,1,0:T(8,128)(2,1)} async-done(((bf16[128,48,1024]{2,1,0:T(8,128)(2,1)}), bf16[128,48,1024]{2,1,0:T(8,128)(2,1)}, u32[]{:S(2)}, u32[]{:S(2)}) %all-to-all-start.2) | async-done | bytes 12582944 | tf_op jit(solution)/shard_map/all_to_all | solution.py:139
  504.6 15.4 %all-to-all-start.4 = ((bf16[128,24,1024]{2,1,0:T(8,128)(2,1)}), bf16[128,24,1024]{2,1,0:T(8,128)(2,1)}, u32[]{:S(2)}, u32[]{:S(2)}) async-start(bf16[128,24,1024]{2,1,0:T(8,128)(2,1)} %bitcast.45), calls=%async_computation.4 | async-start | bytes 12582912 | tf_op jit(solution)/shard_map/all_to_all | solution.py:139
  520.0 23.5 %fusion.2 = f32[384,1024,1]{1,0,2:T(8,128)} fusion(pred[128,72,384]{0,2,1:T(32,128)(4,1)} %copy-done.4, bf16[128,48,1024]{2,1,0:T(8,128)(2,1)} %all-to-all-done.2), kind=kOutput, calls=%fused_computation.3 | convolution fusion | flops 4831838208 | bytes 17694720 | tf_op jit(solution)/shard_map/dot_general | solution.py:142
  543.5 52.6 %all-to-all-done.4 = bf16[128,24,1024]{2,1,0:T(8,128)(2,1)} async-done(((bf16[128,24,1024]{2,1,0:T(8,128)(2,1)}), bf16[128,24,1024]{2,1,0:T(8,128)(2,1)}, u32[]{:S(2)}, u32[]{:S(2)}) %all-to-all-start.4) | async-done | bytes 6291488 | tf_op jit(solution)/shard_map/all_to_all | solution.py:139
  596.0 10.1 %bitcast_add_fusion = f32[384,1024]{1,0:T(8,128)} fusion(f32[384,1024,1]{1,0,2:T(8,128)} %fusion.2, pred[128,72,384]{0,2,1:T(32,128)(4,1)} %copy-done.4, bf16[128,24,1024]{2,1,0:T(8,128)(2,1)} %all-to-all-done.4), kind=kOutput, calls=%fused_computation.15 | convolution fusion | flops 2416312320 | bytes 12976128 | tf_op jit(solution)/shard_map/dot_general | solution.py:142
  606.2 0.0 copy-done.1
  (16 shorter events, 0.1 us)
Async XLA Ops:
  0.6 63.9 %copy-start = (bf16[1024,1024]{1,0:T(8,128)(2,1)S(1)}, bf16[1024,1024]{1,0:T(8,128)(2,1)}, u32[]{:S(2)}) copy-start(bf16[1024,1024]{1,0:T(8,128)(2,1)} %param.7) | copy-start | bytes 6291460
  0.6 7.3 %copy-start.8 = (s32[384,16]{0,1:T(8,128)S(1)}, s32[384,16]{0,1:T(8,128)}, u32[]{:S(2)}) copy-start(s32[384,16]{0,1:T(8,128)} %param.9) | copy-start | bytes 73732
  0.7 7.3 %copy-start.9 = (s32[384,8]{0,1:T(8,128)S(1)}, s32[384,8]{0,1:T(8,128)}, u32[]{:S(2)}) copy-start(s32[384,8]{0,1:T(8,128)} %param.10) | copy-start | bytes 36868
  8.0 1.0 copy-start.5
  39.1 37.6 %all-to-all-start.1 = ((s32[128,72,8]{1,2,0:T(8,128)}), s32[128,72,8]{1,2,0:T(8,128)}, u32[]{:S(2)}, u32[]{:S(2)}) async-start(s32[128,72,8]{1,2,0:T(8,128)} %copy.36), calls=%async_computation.1 | async-start | bytes 1048576 | tf_op jit(solution)/shard_map/all_to_all | solution.py:92
  53.8 1.8 copy-start.4
  57.9 6.6 %copy-start.10 = (bf16[384,1024]{1,0:T(8,128)(2,1)S(1)}, bf16[384,1024]{1,0:T(8,128)(2,1)}, u32[]{:S(2)}) copy-start(bf16[384,1024]{1,0:T(8,128)(2,1)} %param.6) | copy-start | bytes 2359300
  64.6 2.2 copy-start.6
  64.6 2.2 copy-start.11
  65.6 1.1 copy-start.7
  76.7 170.9 %all-to-all-start = ((bf16[128,48,1024]{2,1,0:T(8,128)(2,1)}), bf16[128,48,1024]{2,1,0:T(8,128)(2,1)}, u32[]{:S(2)}, u32[]{:S(2)}) async-start(bf16[128,48,1024]{2,1,0:T(8,128)(2,1)} %bitcast.48), calls=%async_computation | async-start | bytes 25165824 | tf_op jit(solution)/shard_map/all_to_all | solution.py:106
  247.6 91.0 %all-to-all-start.3 = ((bf16[128,24,1024]{2,1,0:T(8,128)(2,1)}), bf16[128,24,1024]{2,1,0:T(8,128)(2,1)}, u32[]{:S(2)}, u32[]{:S(2)}) async-start(bf16[128,24,1024]{2,1,0:T(8,128)(2,1)} %bitcast.53), calls=%async_computation.3 | async-start | bytes 12582912 | tf_op jit(solution)/shard_map/all_to_all | solution.py:106
  268.3 14.8 %copy-start.2 = (s32[72,128,8]{2,1,0:T(8,128)S(1)}, s32[72,128,8]{2,1,0:T(8,128)}, u32[]{:S(2)}) copy-start(s32[72,128,8]{2,1,0:T(8,128)} %copy.37) | copy-start | bytes 884740
  338.6 166.0 %all-to-all-start.2 = ((bf16[128,48,1024]{2,1,0:T(8,128)(2,1)}), bf16[128,48,1024]{2,1,0:T(8,128)(2,1)}, u32[]{:S(2)}, u32[]{:S(2)}) async-start(bf16[128,48,1024]{2,1,0:T(8,128)(2,1)} %bitcast.44), calls=%async_computation.2 | async-start | bytes 25165824 | tf_op jit(solution)/shard_map/all_to_all | solution.py:139
  353.2 2.3 copy-start.3
  504.6 91.4 %all-to-all-start.4 = ((bf16[128,24,1024]{2,1,0:T(8,128)(2,1)}), bf16[128,24,1024]{2,1,0:T(8,128)(2,1)}, u32[]{:S(2)}, u32[]{:S(2)}) async-start(bf16[128,24,1024]{2,1,0:T(8,128)(2,1)} %bitcast.45), calls=%async_computation.4 | async-start | bytes 12582912 | tf_op jit(solution)/shard_map/all_to_all | solution.py:139
  596.0 10.1 %copy-start.1 = (bf16[1024,1024]{1,0:T(8,128)(2,1)S(1)}, bf16[1024,1024]{1,0:T(8,128)(2,1)}, u32[]{:S(2)}) copy-start(bf16[1024,1024]{1,0:T(8,128)(2,1)} %param.7) | copy-start | bytes 6291460

commit v6 on v5

--- a/solution.py
+++ b/solution.py
@@ -6,7 +6,7 @@
 from jax.experimental.pallas import tpu as pltpu
 
 CAP = 6
-CHUNKS = (8, 4)
+CHUNKS = (4, 8)
 AXES = ("row", "col")
 
 
@@ -37,7 +37,7 @@
     rows_ref[...] = jnp.dot(signal, block, preferred_element_type=jnp.float32).astype(jnp.bfloat16)
 
 
-def on_device(pooled, enc_weight, norm_gain, shortlist, positives, label_weight):
+def step(pooled, enc_weight, norm_gain, shortlist, positives, label_weight):
     queries = encode(pooled, enc_weight, norm_gain)
     devices = lax.axis_size("row") * lax.axis_size("col")
     query_count, width = queries.shape
@@ -89,10 +89,6 @@
     inside = (offsets >= 0) & (offsets < block_labels) & occupied
     local_positive = jnp.where(inside, offsets, -1).astype(jnp.int32)
 
-    incoming_pos = lax.all_to_all(
-        local_positive.reshape(devices, per_dst, positive_count),
-        AXES, split_axis=0, concat_axis=0, tiled=True,
-    ).transpose(1, 0, 2).reshape(slots, positive_count)
     by_cluster = jnp.transpose(label_weight, (1, 0, 2))
     rows_per_cluster = CAP * devices
     dispatch = dispatch.reshape(devices, per_dst, query_count)
@@ -105,7 +101,15 @@
         outgoing = jnp.dot(part, queries, preferred_element_type=jnp.float32).astype(jnp.bfloat16)
         incoming = lax.all_to_all(
             outgoing.reshape(devices, rows, width), AXES, split_axis=0, concat_axis=0, tiled=True
-        ).transpose(1, 0, 2).reshape(devices * rows, width)
+        )
+        if first == 0:
+            local_positive, incoming = lax.optimization_barrier((local_positive, incoming))
+            incoming_pos = lax.all_to_all(
+                local_positive.reshape(devices, per_dst, positive_count),
+                AXES, split_axis=0, concat_axis=0, tiled=True,
+            )
+            incoming_pos = incoming_pos.transpose(1, 0, 2).reshape(slots, positive_count)
+        incoming = incoming.transpose(1, 0, 2).reshape(devices * rows, width)
         operands = [incoming, incoming_pos, by_cluster]
         aliases = {}
         if grad is not None:
@@ -157,6 +161,4 @@
         P(None, AXES, None),
     )
     out_specs = (P(AXES, None), P(None, AXES, None))
-    return jax.shard_map(
-        on_device, mesh=mesh, in_specs=in_specs, out_specs=out_specs, check_vma=False
-    )
+    return jax.shard_map(step, mesh=mesh, in_specs=in_specs, out_specs=out_specs, check_vma=False)

time: 616 us -> 645 us (1.047)
  the two profiles are of different devices: /device:TPU:2 before, /device:TPU:10 now
where the time goes in v6:
time: 645 us; the launch traced here: 635 us
  waiting for transfers between devices  363 us (56%)
  local copies, waits for them, and re-layouts  92.5 us (14%)
  starting transfers between devices  63.4 us (10%)
  matrix products  62.4 us (10%)
  Pallas kernels  43.3 us (7%)
  other arithmetic  8.47 us (1%)
    all_to_all x2, waiting for transfers between devices, step(): lax.all_to_all(row_grads, AXES, split_axis=0, concat_axis=0, tiled=True)  199 us
    all_to_all x2, waiting for transfers between devices, step(): lax.all_to_all(outgoing.reshape(devices, rows, width), AXES, split_axis=0...  165 us
    pallas_call x2, Pallas kernels, step(): pl.pallas_call(cluster_kernel, grid=(count,), in_specs=[pl.BlockSpec((row...  43.3 us
    dot_general x2, matrix products, step(): lax.dot_general(part, returned, (((0,), (0,)), ((), ())), preferred_eleme...  33.5 us
    all_to_all x2, starting transfers between devices, step(): lax.all_to_all(row_grads, AXES, split_axis=0, concat_axis=0, tiled=True)  32.7 us
    transpose x2, local copies, waits for them, and re-layouts, step(): incoming = incoming.transpose(1, 0, 2).reshape(devices * rows, width)  23.7 us
    reshape x2, local copies, waits for them, and re-layouts, step(): row_grads = row_grads.reshape(rows, devices, width).transpose(1, 0, 2)  23.6 us
    all_to_all x2, starting transfers between devices, step(): lax.all_to_all(outgoing.reshape(devices, rows, width), AXES, split_axis=0...  21.7 us
  transfers between devices with their start and end apart: 5, of which 4 were waited for; matrix products, arithmetic and copies ran while one was open for 15% of the time, Pallas kernels for 2%

profile of v6, /device:TPU:10, one launch (start us, length us, event | category | flops | bytes accessed | tf_op | source)
XLA Modules:
  0.0 634.6 jit_solution(13525835077965078076)
XLA Ops:
  0.6 0.0 copy-start
  0.7 0.1 eq.69
  0.8 5.7 compare_reduce_fusion
  6.5 1.8 fusion.7
  8.2 2.3 copy.44
  10.5 0.0 copy-done
  10.5 2.2 fusion.27
  12.7 0.0 copy-start.5
  12.7 0.3 multiply_reduce_fusion
  13.0 0.8 copy-done.5
  13.9 1.9 bitcast_compare_fusion
  15.8 0.0 copy-start.3
  15.8 1.7 copy-done.3
  17.5 0.0 copy-start.8
  17.5 0.5 slice.33
  18.0 2.0 copy.34
  20.0 0.0 copy-done.8
  20.0 7.0 %convolution_convert_fusion.1 = bf16[3072,1024]{1,0:T(8,128)(2,1)} fusion(pred[3072,384]{1,0:T(8,128)(4,1)S(1)} %bitcast.61, f32[384,1024]{1,0:T(8,128)} %copy-done.5, f32[1024]{0:T(1024)S(1)} %copy-done.8, f32[384]{0:T(512)S(1)} %add_rsqrt_fusion, f32[384]{0:T(512)S(1)} %broadcast_multiply_fusion.1), kind=kOutput, calls=%fused_computation.11 | convolution fusion | flops 2420637696 | bytes 9051136 | tf_op jit(solution)/shard_map/dot_general | solution.py:101
  27.0 0.0 copy-start.4
  27.0 11.2 %all-to-all-start = ((bf16[128,24,1024]{2,1,0:T(8,128)(2,1)}), bf16[128,24,1024]{2,1,0:T(8,128)(2,1)}, u32[]{:S(2)}, u32[]{:S(2)}) async-start(bf16[128,24,1024]{2,1,0:T(8,128)(2,1)} %bitcast.52), calls=%async_computation | async-start | bytes 12582912 | tf_op jit(solution)/shard_map/all_to_all | solution.py:102
  38.2 0.0 copy-done.4
  38.2 0.7 copy.32
  39.0 3.2 slice.34
  42.1 0.1 eq.73
  42.2 0.5 eq.74
  42.7 6.5 %copy.40 = pred[128,48,384]{2,1,0:T(8,128)(4,1)} copy(pred[128,48,384]{0,2,1:T(8,128)(4,1)} %slice.34) | data formatting | bytes 4718592 | tf_op jit(solution)/shard_map/slice | solution.py:100
  49.2 5.3 eq.66
  54.6 0.0 copy-start.6
  54.6 0.0 copy-start.7
  54.6 12.6 %eq.72 = bf16[9216,384]{1,0:T(8,128)(2,1)} reshape(bf16[128,12,6,384]{3,2,1,0:T(8,128)(2,1)} %eq.66) | data formatting | bytes 14155776 | tf_op jit(solution)/shard_map/eq | solution.py:64
  67.2 0.0 copy-done.6
  67.3 0.0 copy-done.7
  67.3 6.2 fusion
  73.6 0.1 compare_reduce_fusion.1
  73.7 0.2 select_reduce_fusion
  73.9 0.1 and_select_fusion
  74.1 36.0 %all-to-all-done = bf16[128,24,1024]{2,1,0:T(8,128)(2,1)} async-done(((bf16[128,24,1024]{2,1,0:T(8,128)(2,1)}), bf16[128,24,1024]{2,1,0:T(8,128)(2,1)}, u32[]{:S(2)}, u32[]{:S(2)}) %all-to-all-start) | async-done | bytes 6291488 | tf_op jit(solution)/shard_map/all_to_all | solution.py:102
  110.0 0.5 reshape.110
  110.5 1.1 copy.36
  111.6 8.9 %all-to-all-start.1 = ((s32[128,72,8]{1,2,0:T(8,128)}), s32[128,72,8]{1,2,0:T(8,128)S(1)}, u32[]{:S(2)}, u32[]{:S(2)}) async-start(s32[128,72,8]{1,2,0:T(8,128)} %copy.36), calls=%async_computation.1 | async-start | bytes 1048576 | tf_op jit(solution)/shard_map/all_to_all | solution.py:107
  120.6 11.7 %convolution_convert_fusion = bf16[6144,1024]{1,0:T(8,128)(2,1)} fusion(pred[6144,384]{1,0:T(8,128)(4,1)} %bitcast.59, f32[384,1024]{1,0:T(8,128)} %copy-done.5, f32[1024]{0:T(1024)S(1)} %copy-done.8, f32[384]{0:T(512)S(1)} %add_rsqrt_fusion, f32[384]{0:T(512)S(1)} %broadcast_multiply_fusion.1), kind=kOutput, calls=%fused_computation.6 | convolution fusion | flops 4839702528 | bytes 16522240 | tf_op jit(solution)/shard_map/dot_general | solution.py:101
  132.3 0.0 all-to-all-done.1
  132.3 10.6 %all-to-all-start.3 = ((bf16[128,48,1024]{2,1,0:T(8,128)(2,1)}), bf16[128,48,1024]{2,1,0:T(8,128)(2,1)}, u32[]{:S(2)}, u32[]{:S(2)}) async-start(bf16[128,48,1024]{2,1,0:T(8,128)(2,1)} %bitcast.49), calls=%async_computation.3 | async-start | bytes 25165824 | tf_op jit(solution)/shard_map/all_to_all | solution.py:102
  142.9 9.0 %copy.35 = bf16[24,128,1024]{2,1,0:T(8,128)(2,1)} copy(bf16[24,128,1024]{2,0,1:T(8,128)(2,1)} %bitcast.7) | data formatting | bytes 12582912 | tf_op jit(solution)/shard_map/transpose | solution.py:112
  151.9 4.9 copy.37
  156.8 0.0 copy-start.2
  156.8 2.3 copy-done.2
  159.1 15.2 %shard_map.77 = (f32[12,256,1024]{2,1,0:T(8,128)}, bf16[3072,1024]{1,0:T(8,128)(2,1)}) custom-call(bf16[3072,1024]{1,0:T(8,128)(2,1)} %bitcast.54, s32[9216,8]{1,0:T(8,128)S(1)} %bitcast.42, bf16[12,256,1024]{2,1,0:T(8,128)(2,1)} %bitcast.55), custom_call_target="tpu_custom_call" | custom-call | flops 4831838208 | bytes 18874368 | tf_op jit(solution)/shard_map/pallas_call | solution.py:118
  174.3 128.8 %all-to-all-done.3 = bf16[128,48,1024]{2,1,0:T(8,128)(2,1)} async-done(((bf16[128,48,1024]{2,1,0:T(8,128)(2,1)}), bf16[128,48,1024]{2,1,0:T(8,128)(2,1)}, u32[]{:S(2)}, u32[]{:S(2)}) %all-to-all-start.3) | async-done | bytes 12582944 | tf_op jit(solution)/shard_map/all_to_all | solution.py:102
  303.1 0.0 slice-start.1
  303.1 14.7 %copy.41 = bf16[48,128,1024]{2,1,0:T(8,128)(2,1)} copy(bf16[48,128,1024]{2,0,1:T(8,128)(2,1)} %bitcast.17) | data formatting | bytes 25165824 | tf_op jit(solution)/shard_map/transpose | solution.py:112
  317.8 0.0 slice-done
  317.8 0.0 slice-done.1
  317.8 28.1 %shard_map.78 = (f32[12,256,1024]{2,1,0:T(8,128)}, bf16[6144,1024]{1,0:T(8,128)(2,1)}) custom-call(bf16[6144,1024]{1,0:T(8,128)(2,1)} %bitcast.47, s32[9216,8]{1,0:T(8,128)S(1)} %bitcast.45, bf16[12,256,1024]{2,1,0:T(8,128)(2,1)} %bitcast.56, f32[12,256,1024]{2,1,0:T(8,128)} %get-tuple-element.11.refs_0_), custom_call_target="tpu_custom_call", output_to_operand_aliasing={{0}: (3, {})} | custom-call | flops 9663676416 | bytes 37748736 | tf_op jit(solution)/shard_map/pallas_call | solution.py:118
  346.0 14.6 %copy.54 = bf16[48,128,1024]{2,0,1:T(8,128)(2,1)} copy(bf16[48,128,1024]{2,1,0:T(8,128)(2,1)} %bitcast.51) | data formatting | bytes 25165824 | tf_op jit(solution)/shard_map/reshape | solution.py:142
  360.6 15.1 %all-to-all-start.4 = ((bf16[128,48,1024]{2,1,0:T(8,128)(2,1)}), bf16[128,48,1024]{2,1,0:T(8,128)(2,1)}, u32[]{:S(2)}, u32[]{:S(2)}) async-start(bf16[128,48,1024]{2,1,0:T(8,128)(2,1)} %bitcast.46), calls=%async_computation.4 | async-start | bytes 25165824 | tf_op jit(solution)/shard_map/all_to_all | solution.py:143
  375.6 9.0 %copy.55 = bf16[24,128,1024]{2,0,1:T(8,128)(2,1)} copy(bf16[24,128,1024]{2,1,0:T(8,128)(2,1)} %bitcast.53) | data formatting | bytes 12582912 | tf_op jit(solution)/shard_map/reshape | solution.py:142
  384.6 150.2 %all-to-all-done.4 = bf16[128,48,1024]{2,1,0:T(8,128)(2,1)} async-done(((bf16[128,48,1024]{2,1,0:T(8,128)(2,1)}), bf16[128,48,1024]{2,1,0:T(8,128)(2,1)}, u32[]{:S(2)}, u32[]{:S(2)}) %all-to-all-start.4) | async-done | bytes 12582944 | tf_op jit(solution)/shard_map/all_to_all | solution.py:143
  534.9 17.6 %all-to-all-start.2 = ((bf16[128,24,1024]{2,1,0:T(8,128)(2,1)}), bf16[128,24,1024]{2,1,0:T(8,128)(2,1)}, u32[]{:S(2)}, u32[]{:S(2)}) async-start(bf16[128,24,1024]{2,1,0:T(8,128)(2,1)} %bitcast.48), calls=%async_computation.2 | async-start | bytes 12582912 | tf_op jit(solution)/shard_map/all_to_all | solution.py:143
  552.5 23.5 %fusion.2 = f32[384,1024,1]{1,0,2:T(8,128)} fusion(pred[128,72,384]{0,2,1:T(32,128)(4,1)} %copy-done.3, bf16[128,48,1024]{2,1,0:T(8,128)(2,1)} %all-to-all-done.4), kind=kOutput, calls=%fused_computation.3 | convolution fusion | flops 4831838208 | bytes 17694720 | tf_op jit(solution)/shard_map/dot_general | solution.py:146
  576.0 48.4 %all-to-all-done.2 = bf16[128,24,1024]{2,1,0:T(8,128)(2,1)} async-done(((bf16[128,24,1024]{2,1,0:T(8,128)(2,1)}), bf16[128,24,1024]{2,1,0:T(8,128)(2,1)}, u32[]{:S(2)}, u32[]{:S(2)}) %all-to-all-start.2) | async-done | bytes 6291488 | tf_op jit(solution)/shard_map/all_to_all | solution.py:143
  624.3 0.0 copy-start.1
  624.3 10.0 %bitcast_add_fusion = f32[384,1024]{1,0:T(8,128)} fusion(f32[384,1024,1]{1,0,2:T(8,128)} %fusion.2, pred[128,72,384]{0,2,1:T(32,128)(4,1)} %copy-done.3, bf16[128,24,1024]{2,1,0:T(8,128)(2,1)} %all-to-all-done.2), kind=kOutput, calls=%fused_computation.15 | convolution fusion | flops 2416312320 | bytes 12976128 | tf_op jit(solution)/shard_map/dot_general | solution.py:146
  634.3 0.0 copy-done.1
  (15 shorter events, 0.1 us)
Async XLA Ops:
  0.6 9.9 %copy-start = (bf16[1024,1024]{1,0:T(8,128)(2,1)S(1)}, bf16[1024,1024]{1,0:T(8,128)(2,1)}, u32[]{:S(2)}) copy-start(bf16[1024,1024]{1,0:T(8,128)(2,1)} %param.7) | copy-start | bytes 6291460
  12.7 1.1 copy-start.5
  15.8 1.7 copy-start.3
  17.5 2.5 copy-start.8
  27.0 11.2 %copy-start.4 = (bf16[1536,384]{1,0:T(8,128)(2,1)S(1)}, bf16[1536,384]{1,0:T(8,128)(2,1)}, u32[]{:S(2)}) copy-start(bf16[1536,384]{1,0:T(8,128)(2,1)} %fusion.7) | copy-start | bytes 3538948
  27.0 83.0 %all-to-all-start = ((bf16[128,24,1024]{2,1,0:T(8,128)(2,1)}), bf16[128,24,1024]{2,1,0:T(8,128)(2,1)}, u32[]{:S(2)}, u32[]{:S(2)}) async-start(bf16[128,24,1024]{2,1,0:T(8,128)(2,1)} %bitcast.52), calls=%async_computation | async-start | bytes 12582912 | tf_op jit(solution)/shard_map/all_to_all | solution.py:102
  54.6 12.6 %copy-start.6 = (s32[384,16]{0,1:T(8,128)S(1)}, s32[384,16]{0,1:T(8,128)}, u32[]{:S(2)}) copy-start(s32[384,16]{0,1:T(8,128)} %param.9) | copy-start | bytes 73732
  54.6 12.7 %copy-start.7 = (s32[384,8]{0,1:T(8,128)S(1)}, s32[384,8]{0,1:T(8,128)}, u32[]{:S(2)}) copy-start(s32[384,8]{0,1:T(8,128)} %param.10) | copy-start | bytes 36868
  111.6 20.7 %all-to-all-start.1 = ((s32[128,72,8]{1,2,0:T(8,128)}), s32[128,72,8]{1,2,0:T(8,128)S(1)}, u32[]{:S(2)}, u32[]{:S(2)}) async-start(s32[128,72,8]{1,2,0:T(8,128)} %copy.36), calls=%async_computation.1 | async-start | bytes 1048576 | tf_op jit(solution)/shard_map/all_to_all | solution.py:107
  132.3 170.8 %all-to-all-start.3 = ((bf16[128,48,1024]{2,1,0:T(8,128)(2,1)}), bf16[128,48,1024]{2,1,0:T(8,128)(2,1)}, u32[]{:S(2)}, u32[]{:S(2)}) async-start(bf16[128,48,1024]{2,1,0:T(8,128)(2,1)} %bitcast.49), calls=%async_computation.3 | async-start | bytes 25165824 | tf_op jit(solution)/shard_map/all_to_all | solution.py:102
  156.8 2.3 copy-start.2
  159.1 158.7 %slice-start = ((s8[4718592]{0:T(1024)(128)(4,1)}), s8[524288]{0:T(1024)(128)(4,1)S(1)}, s32[]{:S(2)}) async-start(s8[4718592]{0:T(1024)(128)(4,1)} %bitcast.43), calls=%async_computation.5 | async-start | bytes 1048576
  303.1 14.7 %slice-start.1 = ((s8[4718592]{0:T(1024)(128)(4,1)}), s8[4194304]{0:T(1024)(128)(4,1)S(1)}, s32[]{:S(2)}) async-start(s8[4718592]{0:T(1024)(128)(4,1)} %bitcast.43), calls=%async_computation.6 | async-start | bytes 8388608
  360.6 174.3 %all-to-all-start.4 = ((bf16[128,48,1024]{2,1,0:T(8,128)(2,1)}), bf16[128,48,1024]{2,1,0:T(8,128)(2,1)}, u32[]{:S(2)}, u32[]{:S(2)}) async-start(bf16[128,48,1024]{2,1,0:T(8,128)(2,1)} %bitcast.46), calls=%async_computation.4 | async-start | bytes 25165824 | tf_op jit(solution)/shard_map/all_to_all | solution.py:143
  534.9 89.5 %all-to-all-start.2 = ((bf16[128,24,1024]{2,1,0:T(8,128)(2,1)}), bf16[128,24,1024]{2,1,0:T(8,128)(2,1)}, u32[]{:S(2)}, u32[]{:S(2)}) async-start(bf16[128,24,1024]{2,1,0:T(8,128)(2,1)} %bitcast.48), calls=%async_computation.2 | async-start | bytes 12582912 | tf_op jit(solution)/shard_map/all_to_all | solution.py:143
  624.3 10.0 %copy-start.1 = (bf16[1024,1024]{1,0:T(8,128)(2,1)S(1)}, bf16[1024,1024]{1,0:T(8,128)(2,1)}, u32[]{:S(2)}) copy-start(bf16[1024,1024]{1,0:T(8,128)(2,1)} %param.7) | copy-start | bytes 6291460

commit v7 on v6

--- a/solution.py
+++ b/solution.py
@@ -6,7 +6,7 @@
 from jax.experimental.pallas import tpu as pltpu
 
 CAP = 6
-CHUNKS = (4, 8)
+CHUNKS = (8, 4)
 AXES = ("row", "col")
 
 
@@ -91,13 +91,17 @@
 
     by_cluster = jnp.transpose(label_weight, (1, 0, 2))
     rows_per_cluster = CAP * devices
-    dispatch = dispatch.reshape(devices, per_dst, query_count)
     query_grad = jnp.zeros((query_count, width), jnp.float32)
     grad = None
     first = 0
     for count in CHUNKS:
         rows = count * CAP
-        part = dispatch[:, first * CAP : first * CAP + rows, :].reshape(devices * rows, query_count)
+        part = (
+            (level[first : first + count] == slot_rank)
+            .astype(jnp.bfloat16)
+            .transpose(2, 0, 1, 3)
+            .reshape(devices * rows, query_count)
+        )
         outgoing = jnp.dot(part, queries, preferred_element_type=jnp.float32).astype(jnp.bfloat16)
         incoming = lax.all_to_all(
             outgoing.reshape(devices, rows, width), AXES, split_axis=0, concat_axis=0, tiled=True

time: 645 us -> 665 us (1.031)
  the two profiles are of different devices: /device:TPU:10 before, /device:TPU:90 now
where the time goes in v7:
time: 665 us; the launch traced here: 656 us
  waiting for transfers between devices  397 us (60%)
  local copies, waits for them, and re-layouts  110 us (17%)
  starting transfers between devices  47.7 us (7%)
  matrix products  44.5 us (7%)
  Pallas kernels  43.3 us (7%)
  other arithmetic  12.1 us (2%)
    all_to_all x2, waiting for transfers between devices, step(): lax.all_to_all(row_grads, AXES, split_axis=0, concat_axis=0, tiled=True)  203 us
    all_to_all x2, waiting for transfers between devices, step(): lax.all_to_all(outgoing.reshape(devices, rows, width), AXES, split_axis=0...  194 us
    pallas_call x2, Pallas kernels, step(): pl.pallas_call(cluster_kernel, grid=(count,), in_specs=[pl.BlockSpec((row...  43.3 us
    eq x12, local copies, waits for them, and re-layouts, step(): level[first:first + count] == slot_rank  31.7 us
    reshape x2, local copies, waits for them, and re-layouts, step(): row_grads = row_grads.reshape(rows, devices, width).transpose(1, 0, 2)  23.6 us
    transpose x2, local copies, waits for them, and re-layouts, step(): incoming = incoming.transpose(1, 0, 2).reshape(devices * rows, width)  23.6 us
    eq x5, local copies, waits for them, and re-layouts, step(): level == slot_rank  20.5 us
    dot_general x2, matrix products, step(): jnp.dot(part, queries, preferred_element_type=jnp.float32)  19.9 us
  transfers between devices with their start and end apart: 5, of which 4 were waited for; matrix products, arithmetic and copies ran while one was open for 16% of the time, Pallas kernels for 0%

profile of v7, /device:TPU:90, one launch (start us, length us, event | category | flops | bytes accessed | tf_op | source)
XLA Modules:
  0.0 656.2 jit_solution(16916088871400392689)
XLA Ops:
  0.6 0.0 copy-start
  0.6 0.0 copy-start.9
  0.7 5.7 compare_reduce_fusion
  6.4 0.8 fusion.5
  7.2 0.0 copy-done
  7.2 0.0 copy-done.9
  7.2 0.0 copy-start.3
  7.2 1.1 fusion.25
  8.3 1.1 copy-done.4
  9.4 0.3 multiply_reduce_fusion
  9.8 0.4 eq.147
  10.2 0.0 copy-done.3
  10.2 0.1 slice.30
  10.3 0.5 copy.32
  10.7 4.2 eq.131
  14.9 9.2 %eq.145 = bf16[6144,384]{1,0:T(8,128)(2,1)} reshape(bf16[128,8,6,384]{3,2,1,0:T(8,128)(2,1)} %eq.131) | data formatting | bytes 9437184 | tf_op jit(solution)/shard_map/eq | solution.py:100
  24.1 0.0 copy-done.5
  24.1 0.0 copy-done.10
  24.1 11.8 %convolution_convert_fusion = bf16[6144,1024]{1,0:T(8,128)(2,1)} fusion(bf16[6144,384]{1,0:T(8,128)(2,1)} %eq.145, bf16[6144]{0:T(1024)(128)(2,1)S(1)} %eq.147, f32[384,1024]{1,0:T(8,128)S(1)} %copy-done.5, f32[1024]{0:T(1024)S(1)} %copy-done.10, f32[384]{0:T(512)S(1)} %add_rsqrt_fusion, f32[384]{0:T(512)S(1)} %broadcast_multiply_fusion.1), kind=kOutput, calls=%fused_computation.4 | convolution fusion | flops 4842061824 | bytes 18893824 | tf_op jit(solution)/shard_map/dot_general | solution.py:105
  35.9 10.3 %all-to-all-start = ((bf16[128,48,1024]{2,1,0:T(8,128)(2,1)}), bf16[128,48,1024]{2,1,0:T(8,128)(2,1)}, u32[]{:S(2)}, u32[]{:S(2)}) async-start(bf16[128,48,1024]{2,1,0:T(8,128)(2,1)} %bitcast.48), calls=%async_computation | async-start | bytes 25165824 | tf_op jit(solution)/shard_map/all_to_all | solution.py:106
  46.3 0.2 eq.158
  46.5 0.0 slice-done
  46.5 0.3 copy.38
  46.8 2.2 eq.152
  49.0 5.2 eq.156
  54.1 8.1 %convolution_convert_fusion.1 = bf16[3072,1024]{1,0:T(8,128)(2,1)} fusion(bf16[3072,384]{1,0:T(8,128)(2,1)} %eq.156, bf16[3072]{0:T(1024)(128)(2,1)S(1)} %eq.158, f32[384,1024]{1,0:T(8,128)S(1)} %copy-done.5, f32[1024]{0:T(1024)S(1)} %copy-done.10, f32[384]{0:T(512)S(1)} %add_rsqrt_fusion, f32[384]{0:T(512)S(1)} %broadcast_multiply_fusion.1), kind=kOutput, calls=%fused_computation.7 | convolution fusion | flops 2421817344 | bytes 10236928 | tf_op jit(solution)/shard_map/dot_general | solution.py:105
  62.2 152.2 %all-to-all-done = bf16[128,48,1024]{2,1,0:T(8,128)(2,1)} async-done(((bf16[128,48,1024]{2,1,0:T(8,128)(2,1)}), bf16[128,48,1024]{2,1,0:T(8,128)(2,1)}, u32[]{:S(2)}, u32[]{:S(2)}) %all-to-all-start) | async-done | bytes 12582944 | tf_op jit(solution)/shard_map/all_to_all | solution.py:106
  214.4 8.8 %all-to-all-start.3 = ((bf16[128,24,1024]{2,1,0:T(8,128)(2,1)}), bf16[128,24,1024]{2,1,0:T(8,128)(2,1)}, u32[]{:S(2)}, u32[]{:S(2)}) async-start(bf16[128,24,1024]{2,1,0:T(8,128)(2,1)} %bitcast.53), calls=%async_computation.3 | async-start | bytes 12582912 | tf_op jit(solution)/shard_map/all_to_all | solution.py:106
  223.2 0.1 eq.139
  223.3 0.5 eq.140
  223.8 2.0 copy.33
  225.8 5.3 eq.137
  231.1 12.6 %eq.138 = bf16[9216,384]{1,0:T(8,128)(2,1)} reshape(bf16[128,12,6,384]{3,2,1,0:T(8,128)(2,1)} %eq.137) | data formatting | bytes 14155776 | tf_op jit(solution)/shard_map/eq | solution.py:64
  243.7 0.0 copy-done.7
  243.8 0.0 copy-done.8
  243.8 6.2 fusion
  250.1 0.1 compare_reduce_fusion.1
  250.2 0.2 select_reduce_fusion
  250.4 0.9 and_select_fusion
  251.3 1.4 reshape.175
  252.7 1.1 copy.35
  253.8 41.5 %all-to-all-done.3 = bf16[128,24,1024]{2,1,0:T(8,128)(2,1)} async-done(((bf16[128,24,1024]{2,1,0:T(8,128)(2,1)}), bf16[128,24,1024]{2,1,0:T(8,128)(2,1)}, u32[]{:S(2)}, u32[]{:S(2)}) %all-to-all-start.3) | async-done | bytes 6291488 | tf_op jit(solution)/shard_map/all_to_all | solution.py:106
  295.3 9.0 %all-to-all-start.1 = ((s32[128,72,8]{1,2,0:T(8,128)}), s32[128,72,8]{1,2,0:T(8,128)S(1)}, u32[]{:S(2)}, u32[]{:S(2)}) async-start(s32[128,72,8]{1,2,0:T(8,128)} %copy.35), calls=%async_computation.1 | async-start | bytes 1048576 | tf_op jit(solution)/shard_map/all_to_all | solution.py:111
  304.3 9.0 %copy.39 = bf16[24,128,1024]{2,1,0:T(8,128)(2,1)} copy(bf16[24,128,1024]{2,0,1:T(8,128)(2,1)} %bitcast.18) | data formatting | bytes 12582912 | tf_op jit(solution)/shard_map/transpose | solution.py:116
  313.3 14.6 %copy.34 = bf16[48,128,1024]{2,1,0:T(8,128)(2,1)} copy(bf16[48,128,1024]{2,0,1:T(8,128)(2,1)} %bitcast.7) | data formatting | bytes 25165824 | tf_op jit(solution)/shard_map/transpose | solution.py:116
  327.9 0.0 all-to-all-done.1
  327.9 4.8 copy.36
  332.7 2.3 copy-done.2
  335.0 27.6 %shard_map.77 = (f32[12,256,1024]{2,1,0:T(8,128)}, bf16[6144,1024]{1,0:T(8,128)(2,1)}) custom-call(bf16[6144,1024]{1,0:T(8,128)(2,1)} %bitcast.50, s32[9216,8]{1,0:T(8,128)S(1)} %bitcast.42, bf16[12,256,1024]{2,1,0:T(8,128)(2,1)} %bitcast.51), custom_call_target="tpu_custom_call" | custom-call | flops 9663676416 | bytes 37748736 | tf_op jit(solution)/shard_map/pallas_call | solution.py:122
  362.6 15.7 %shard_map.78 = (f32[12,256,1024]{2,1,0:T(8,128)}, bf16[3072,1024]{1,0:T(8,128)(2,1)}) custom-call(bf16[3072,1024]{1,0:T(8,128)(2,1)} %bitcast.45, s32[9216,8]{1,0:T(8,128)S(1)} %bitcast.43, bf16[12,256,1024]{2,1,0:T(8,128)(2,1)} %bitcast.52, f32[12,256,1024]{2,1,0:T(8,128)} %get-tuple-element.11.refs_0_), custom_call_target="tpu_custom_call", output_to_operand_aliasing={{0}: (3, {})} | custom-call | flops 4831838208 | bytes 18874368 | tf_op jit(solution)/shard_map/pallas_call | solution.py:122
  378.3 9.0 %copy.44 = bf16[24,128,1024]{2,0,1:T(8,128)(2,1)} copy(bf16[24,128,1024]{2,1,0:T(8,128)(2,1)} %bitcast.54) | data formatting | bytes 12582912 | tf_op jit(solution)/shard_map/reshape | solution.py:146
  387.3 10.2 %all-to-all-start.4 = ((bf16[128,24,1024]{2,1,0:T(8,128)(2,1)}), bf16[128,24,1024]{2,1,0:T(8,128)(2,1)}, u32[]{:S(2)}, u32[]{:S(2)}) async-start(bf16[128,24,1024]{2,1,0:T(8,128)(2,1)} %bitcast.46), calls=%async_computation.4 | async-start | bytes 12582912 | tf_op jit(solution)/shard_map/all_to_all | solution.py:147
  397.4 14.6 %copy.43 = bf16[48,128,1024]{2,0,1:T(8,128)(2,1)} copy(bf16[48,128,1024]{2,1,0:T(8,128)(2,1)} %bitcast.49) | data formatting | bytes 25165824 | tf_op jit(solution)/shard_map/reshape | solution.py:146
  412.1 57.6 %all-to-all-done.4 = bf16[128,24,1024]{2,1,0:T(8,128)(2,1)} async-done(((bf16[128,24,1024]{2,1,0:T(8,128)(2,1)}), bf16[128,24,1024]{2,1,0:T(8,128)(2,1)}, u32[]{:S(2)}, u32[]{:S(2)}) %all-to-all-start.4) | async-done | bytes 6291488 | tf_op jit(solution)/shard_map/all_to_all | solution.py:147
  469.7 9.5 %all-to-all-start.2 = ((bf16[128,48,1024]{2,1,0:T(8,128)(2,1)}), bf16[128,48,1024]{2,1,0:T(8,128)(2,1)}, u32[]{:S(2)}, u32[]{:S(2)}) async-start(bf16[128,48,1024]{2,1,0:T(8,128)(2,1)} %bitcast.44), calls=%async_computation.2 | async-start | bytes 25165824 | tf_op jit(solution)/shard_map/all_to_all | solution.py:147
  479.2 1.2 broadcast_compare_fusion.1
  480.3 2.2 eq.155
  482.5 3.7 broadcast_compare_fusion
  486.2 7.4 %eq.134 = pred[6144,384]{1,0:T(32,128)(4,1)} reshape(pred[128,8,6,384]{3,2,1,0:T(8,128)(4,1)} %broadcast_compare_fusion) | data formatting | bytes 4718592 | tf_op jit(solution)/shard_map/eq | solution.py:100
  493.6 0.0 copy-done.6
  493.6 6.6 %fusion.26 = f32[384,1024]{1,0:T(8,128)} fusion(pred[3072,384]{1,0:T(32,128)(4,1)S(1)} %copy-done.6, bf16[3072,1024]{1,0:T(8,128)(2,1)} %bitcast.22), kind=kOutput, calls=%fused_computation.70 | convolution fusion | flops 2415919104 | bytes 9043968 | tf_op jit(solution)/shard_map/dot_general | solution.py:150
  500.2 145.8 %all-to-all-done.2 = bf16[128,48,1024]{2,1,0:T(8,128)(2,1)} async-done(((bf16[128,48,1024]{2,1,0:T(8,128)(2,1)}), bf16[128,48,1024]{2,1,0:T(8,128)(2,1)}, u32[]{:S(2)}, u32[]{:S(2)}) %all-to-all-start.2) | async-done | bytes 12582944 | tf_op jit(solution)/shard_map/all_to_all | solution.py:147
  646.0 10.0 %convolution_add_fusion = f32[384,1024]{1,0:T(8,128)} fusion(f32[384,1024]{1,0:T(8,128)} %fusion.26, pred[6144,384]{1,0:T(32,128)(4,1)} %eq.134, bf16[6144,1024]{1,0:T(8,128)(2,1)} %bitcast.14), kind=kOutput, calls=%fused_computation.17 | convolution fusion | flops 4832231424 | bytes 18087936 | tf_op jit(solution)/shard_map/dot_general | solution.py:150
  656.1 0.0 copy-done.1
  (23 shorter events, 0.2 us)
Async XLA Ops:
  0.6 6.6 copy-start
  0.6 6.5 copy-start.9
  7.2 3.0 copy-start.3
  8.3 1.1 copy-start.4
  14.9 9.2 %copy-start.5 = (f32[384,1024]{1,0:T(8,128)S(1)}, f32[384,1024]{1,0:T(8,128)}, u32[]{:S(2)}) copy-start(f32[384,1024]{1,0:T(8,128)} %copy-done.4) | copy-start | bytes 4718596
  14.9 9.2 %copy-start.10 = (f32[1024]{0:T(1024)S(1)}, f32[1024]{0:T(1024)}, u32[]{:S(2)}) copy-start(f32[1024]{0:T(1024)} %param.8) | copy-start | bytes 12292
  35.9 10.5 %slice-start = ((bf16[1536,384]{1,0:T(8,128)(2,1)}), bf16[512,384]{1,0:T(8,128)(2,1)S(1)}, s32[]{:S(2)}) async-start(bf16[1536,384]{1,0:T(8,128)(2,1)} %copy-done.3), calls=%async_computation.5 | async-start | bytes 786432 | tf_op jit(solution)/shard_map/slice | solution.py:100
  35.9 178.4 %all-to-all-start = ((bf16[128,48,1024]{2,1,0:T(8,128)(2,1)}), bf16[128,48,1024]{2,1,0:T(8,128)(2,1)}, u32[]{:S(2)}, u32[]{:S(2)}) async-start(bf16[128,48,1024]{2,1,0:T(8,128)(2,1)} %bitcast.48), calls=%async_computation | async-start | bytes 25165824 | tf_op jit(solution)/shard_map/all_to_all | solution.py:106
  214.4 80.9 %all-to-all-start.3 = ((bf16[128,24,1024]{2,1,0:T(8,128)(2,1)}), bf16[128,24,1024]{2,1,0:T(8,128)(2,1)}, u32[]{:S(2)}, u32[]{:S(2)}) async-start(bf16[128,24,1024]{2,1,0:T(8,128)(2,1)} %bitcast.53), calls=%async_computation.3 | async-start | bytes 12582912 | tf_op jit(solution)/shard_map/all_to_all | solution.py:106
  231.1 12.6 %copy-start.7 = (s32[384,16]{0,1:T(8,128)S(1)}, s32[384,16]{0,1:T(8,128)}, u32[]{:S(2)}) copy-start(s32[384,16]{0,1:T(8,128)} %param.9) | copy-start | bytes 73732
  231.1 12.7 %copy-start.8 = (s32[384,8]{0,1:T(8,128)S(1)}, s32[384,8]{0,1:T(8,128)}, u32[]{:S(2)}) copy-start(s32[384,8]{0,1:T(8,128)} %param.10) | copy-start | bytes 36868
  295.3 32.5 %all-to-all-start.1 = ((s32[128,72,8]{1,2,0:T(8,128)}), s32[128,72,8]{1,2,0:T(8,128)S(1)}, u32[]{:S(2)}, u32[]{:S(2)}) async-start(s32[128,72,8]{1,2,0:T(8,128)} %copy.35), calls=%async_computation.1 | async-start | bytes 1048576 | tf_op jit(solution)/shard_map/all_to_all | solution.py:111
  332.7 2.3 copy-start.2
  387.3 82.4 %all-to-all-start.4 = ((bf16[128,24,1024]{2,1,0:T(8,128)(2,1)}), bf16[128,24,1024]{2,1,0:T(8,128)(2,1)}, u32[]{:S(2)}, u32[]{:S(2)}) async-start(bf16[128,24,1024]{2,1,0:T(8,128)(2,1)} %bitcast.46), calls=%async_computation.4 | async-start | bytes 12582912 | tf_op jit(solution)/shard_map/all_to_all | solution.py:147
  469.7 176.3 %all-to-all-start.2 = ((bf16[128,48,1024]{2,1,0:T(8,128)(2,1)}), bf16[128,48,1024]{2,1,0:T(8,128)(2,1)}, u32[]{:S(2)}, u32[]{:S(2)}) async-start(bf16[128,48,1024]{2,1,0:T(8,128)(2,1)} %bitcast.44), calls=%async_computation.2 | async-start | bytes 25165824 | tf_op jit(solution)/shard_map/all_to_all | solution.py:147
  486.2 7.4 %copy-start.6 = (pred[3072,384]{1,0:T(32,128)(4,1)S(1)}, pred[3072,384]{1,0:T(32,128)(4,1)}, u32[]{:S(2)}) copy-start(pred[3072,384]{1,0:T(32,128)(4,1)} %eq.155) | copy-start | bytes 3538948
  646.0 10.0 %copy-start.1 = (bf16[1024,1024]{1,0:T(8,128)(2,1)S(1)}, bf16[1024,1024]{1,0:T(8,128)(2,1)}, u32[]{:S(2)}) copy-start(bf16[1024,1024]{1,0:T(8,128)(2,1)} %param.7) | copy-start | bytes 6291460
